TPU v7x, 256 devices: a whole 4x4x8 slice. The times are simulated.
256 devices in a mesh: comp: 32 (over y, x, core), prompt: 8 (over z).
Axes of the slice: x: 4, y: 4, z: 8, core: 2. Of those that a mesh axis runs over, the one named last changes fastest.
Arguments:
- queries: bfloat16 [65536, 2560], P(('prompt', 'comp')), parts along dimension 0, may hold values from -128 to 128, as said below
- suffix_key_value: bfloat16 [2, 65536, 512], P(None, ('prompt', 'comp')), parts along dimension 1, may hold values from -6 to 6
- output_gradient: bfloat16 [65536, 2560], P(('prompt', 'comp')), parts along dimension 0, may hold values from -96 to 96
- node_kv: bfloat16 [256, 2, 128, 512], P(('prompt', 'comp')), parts along dimension 0, may hold values from -8 to 8, as said below
- paths: int32 [512, 4], P(('prompt', 'comp')), parts along dimension 0, may hold values from 0 to 31, as said below
- tile_lens: int32 [256], P('prompt'), parts along dimension 0, may hold values from 1 to 128, as said below
Outputs:
- query_out: bfloat16 [65536, 2560], P(('prompt', 'comp')), parts along dimension 0
- suffix_out: bfloat16 [2, 65536, 512], P(None, ('prompt', 'comp')), parts along dimension 1
- node_out: bfloat16 [256, 2, 128, 512], P(('prompt', 'comp')), parts along dimension 0
There are 8 independent parts, one for each index of `prompt`. A program takes and returns all parts, laid end to end along the dimension named above; each array names one. Nothing has to cross between parts.
Inputs may be any that keep to these rules, and one draw needn't show every extreme that they name: paths[c] are the 4 trie nodes of completion c from the root down; every completion has the same root, the completions of one block of 2 share their second node, and each node has one parent; node n's tile is row n of node_kv, values are node numbers below 32. `tile_lens`: the root's tile is full. real-valued queries. `node_kv`: real-valued keys and values.
All inputs are finite; a program needn't handle non-finite values.
Results may differ from a plain program's by a relative error of at most 0.02.
Values may be sent and summed in bfloat16 or wider, within the bound.
No kernel may reach another device: no remote copies, remote signals or barrier semaphores. Data moves between devices by JAX's collectives and lax.ppermute only.
A program may use at most 128 MiB of HBM per device.

v0:
```python
import math

import jax
import jax.numpy as jnp
from jax import lax
from jax.sharding import PartitionSpec as P

QUERY_HEADS = 20
KV_HEADS = 4
HEAD_SIZE = 128
TILE_SLOTS = 128
DEPTH = 4
QUERY_LENGTH = 128


def head_block(query_block, cot_block, key_block, value_block, visible, factor):
    scores = (
        jnp.einsum("igd,jd->gij", query_block, key_block, preferred_element_type=jnp.float32)
        * factor
    )
    scores = jnp.where(visible[None], scores, -jnp.inf)
    top_score = jnp.max(scores, axis=-1, keepdims=True)
    weights = jnp.exp(scores - top_score)
    probs = weights / jnp.sum(weights, axis=-1, keepdims=True)
    probs_low = probs.astype(jnp.bfloat16)
    outputs = jnp.einsum("gij,jd->igd", probs_low, value_block, preferred_element_type=jnp.float32)
    centre = jnp.sum(cot_block.astype(jnp.float32) * outputs, axis=-1)
    prob_grads = jnp.einsum(
        "igd,jd->gij", cot_block, value_block, preferred_element_type=jnp.float32
    )
    score_grads = probs * (prob_grads - jnp.transpose(centre)[:, :, None])
    score_low = score_grads.astype(jnp.bfloat16)
    query_gradient = (
        jnp.einsum("gij,jd->igd", score_low, key_block, preferred_element_type=jnp.float32) * factor
    ).astype(jnp.bfloat16)
    key_gradient = (
        jnp.einsum("gij,igd->jd", score_low, query_block, preferred_element_type=jnp.float32)
        * factor
    )
    value_gradient = jnp.einsum(
        "gij,igd->jd", probs_low, cot_block, preferred_element_type=jnp.float32
    )
    return (query_gradient, key_gradient, value_gradient)


def body(queries, suffix_key_value, output_gradient, node_kv, paths, tile_lens):
    members = paths.shape[0]
    span_width = node_kv.shape[-1]
    group_share = QUERY_HEADS // KV_HEADS
    factor = 1.0 / math.sqrt(HEAD_SIZE)
    trie_node_rows = DEPTH * TILE_SLOTS
    blank_tiles = jnp.zeros((members, DEPTH) + node_kv.shape[1:], jnp.bfloat16)
    portion = lax.all_gather(node_kv, "comp", axis=0, tiled=True)
    present = (paths >= 0) & (paths < portion.shape[0])
    fetched = jnp.take(portion, jnp.clip(paths, 0, portion.shape[0] - 1), axis=0)
    path_tiles = jnp.where(present[:, :, None, None, None], fetched, blank_tiles)
    valid_len = jnp.take(tile_lens, paths)
    slot_index = jnp.arange(TILE_SLOTS)
    causal = jnp.arange(QUERY_LENGTH)[None, :] <= jnp.arange(QUERY_LENGTH)[:, None]

    def completion(member_flag):
        query_matrix = lax.dynamic_slice_in_dim(
            queries, member_flag * QUERY_LENGTH, QUERY_LENGTH, 0
        )
        cotangent_rows = lax.dynamic_slice_in_dim(
            output_gradient, member_flag * QUERY_LENGTH, QUERY_LENGTH, 0
        )
        tile_token_block = path_tiles[member_flag]
        suffix_rows = lax.dynamic_slice_in_dim(
            suffix_key_value, member_flag * QUERY_LENGTH, QUERY_LENGTH, 1
        )
        key_matrix = jnp.concatenate(
            [tile_token_block[:, 0].reshape(trie_node_rows, span_width), suffix_rows[0]], axis=0
        )
        value_matrix = jnp.concatenate(
            [tile_token_block[:, 1].reshape(trie_node_rows, span_width), suffix_rows[1]], axis=0
        )
        node_seen = (slot_index[None, :] < valid_len[member_flag][:, None]).reshape(trie_node_rows)
        visible = jnp.concatenate(
            [jnp.broadcast_to(node_seen[None, :], (QUERY_LENGTH, trie_node_rows)), causal], axis=1
        )

        def head_share(head_index):
            query_block = lax.dynamic_slice_in_dim(
                query_matrix, head_index * group_share * HEAD_SIZE, group_share * HEAD_SIZE, 1
            ).reshape(QUERY_LENGTH, group_share, HEAD_SIZE)
            cot_block = lax.dynamic_slice_in_dim(
                cotangent_rows, head_index * group_share * HEAD_SIZE, group_share * HEAD_SIZE, 1
            ).reshape(QUERY_LENGTH, group_share, HEAD_SIZE)
            key_block = lax.dynamic_slice_in_dim(key_matrix, head_index * HEAD_SIZE, HEAD_SIZE, 1)
            value_block = lax.dynamic_slice_in_dim(
                value_matrix, head_index * HEAD_SIZE, HEAD_SIZE, 1
            )
            return head_block(query_block, cot_block, key_block, value_block, visible, factor)

        query_gradient, key_gradient, value_gradient = lax.map(head_share, jnp.arange(KV_HEADS))
        query_gradient = jnp.transpose(query_gradient, (1, 0, 2, 3)).reshape(
            QUERY_LENGTH, QUERY_HEADS * HEAD_SIZE
        )
        key_gradient = jnp.transpose(key_gradient, (1, 0, 2)).reshape(
            trie_node_rows + QUERY_LENGTH, span_width
        )
        value_gradient = jnp.transpose(value_gradient, (1, 0, 2)).reshape(
            trie_node_rows + QUERY_LENGTH, span_width
        )
        return (query_gradient, key_gradient, value_gradient)

    query_gradient, key_gradient, value_gradient = lax.map(completion, jnp.arange(members))
    query_out = query_gradient.reshape(members * QUERY_LENGTH, QUERY_HEADS * HEAD_SIZE)
    suffix_out = (
        jnp.stack([key_gradient[:, trie_node_rows:], value_gradient[:, trie_node_rows:]], axis=0)
        .reshape(2, members * QUERY_LENGTH, span_width)
        .astype(jnp.bfloat16)
    )
    node_terms = jnp.stack(
        [
            key_gradient[:, :trie_node_rows].reshape(members, DEPTH, TILE_SLOTS, span_width),
            value_gradient[:, :trie_node_rows].reshape(members, DEPTH, TILE_SLOTS, span_width),
        ],
        axis=2,
    ).reshape(members * DEPTH, 2 * TILE_SLOTS * span_width)
    node_count = tile_lens.shape[0]
    one_hot = (jnp.arange(node_count)[:, None] == paths.reshape(-1)[None, :]).astype(jnp.float32)
    block_sum = jnp.dot(one_hot, node_terms, precision=lax.Precision.HIGHEST).reshape(
        node_count, 2, TILE_SLOTS, span_width
    )
    node_out = lax.psum_scatter(
        block_sum.astype(jnp.bfloat16), "comp", scatter_dimension=0, tiled=True
    )
    return (query_out, suffix_out, node_out)


def solution(mesh):
    in_specs = (
        P(("prompt", "comp"), None),
        P(None, ("prompt", "comp"), None),
        P(("prompt", "comp"), None),
        P(("prompt", "comp"), None, None, None),
        P(("prompt", "comp"), None),
        P("prompt"),
    )
    out_specs = (
        P(("prompt", "comp"), None),
        P(None, ("prompt", "comp"), None),
        P(("prompt", "comp"), None, None, None),
    )
    return jax.shard_map(body, mesh=mesh, in_specs=in_specs, out_specs=out_specs, check_vma=False)
```

profile of v0, /device:TPU:2, one launch (start us, length us, event | category | flops | bytes accessed | tf_op | source)
XLA Modules:
  0.0 338.1 jit_solution(12321189691579458037)
XLA Ops:
  12.3 59.0 %all-gather.2.cloned.1.call-done = bf16[32,2,128,512]{3,2,1,0:T(8,128)(2,1)} async-done(((bf16[1,2,128,512]{3,2,1,0:T(8,128)(2,1)}), bf16[32,2,128,512]{3,2,1,0:T(8,128)(2,1)}) %all-gather.2.cloned.1.call-update) | async-done | bytes 8388624 | tf_op jit(solution)/shard_map/all_gather | solution.py:53
  71.3 5.5 %gather_fusion = bf16[8,2,128,512]{3,2,1,0:T(8,128)(2,1)} fusion(bf16[32,2,128,512]{3,2,1,0:T(8,128)(2,1)} %all-gather.2.cloned.1.call-done, s32[1024]{0:T(1024)S(1)} %pad_clamp_fusion.1), kind=kCustom, calls=%fused_computation | custom fusion | bytes 4194336 | tf_op jit(solution)/shard_map/jit(_take)/gather | solution.py:55
  76.8 1.9 select_select_fusion
  78.7 120.9 %while.48 = (s32[]{:T(128)}, bf16[2,128,2560]{2,1,0:T(8,128)(2,1)}, f32[2,640,512]{2,1,0:T(8,128)}, f32[2,640,512]{2,1,0:T(8,128)}, s32[2]{0:T(128)S(1)}, /*inde...) while((s32[]{:T(128)}, bf16[2,128,2560]{2,1,0:T(8,128)(2,1)}, ...), condition=%wide.region_6.7_spmd.clone, body=%wide.region_0.6_spmd.clone.sunk | while | flops 636453376 | bytes 75320104 | solution.py:108
  82.9 1.6 dynamic-slice_bitcast_fusion.3
  88.5 39.8 %while.49 = (s32[]{:T(128)}, bf16[4,128,5,128]{1,3,2,0:T(8,128)(2,1)}, f32[4,640,128]{2,1,0:T(8,128)}, f32[4,640,128]{2,1,0:T(8,128)}, s32[4]{0:T(128)S(1)}, /*i...) while((s32[]{:T(128)}, ...), condition=%wide.region_5.5_spmd, body=%wide.region_1.4_spmd.sunk | while | flops 633733120 | bytes 16154433 | solution.py:96
  95.4 1.9 fusion.97
  100.7 1.6 exponential_reduce_fusion.2
  105.4 1.9 fusion.97
  110.6 1.6 exponential_reduce_fusion.2
  115.3 1.9 fusion.97
  120.6 1.6 exponential_reduce_fusion.2
  125.3 1.9 fusion.97
  128.3 2.2 copy.79
  135.8 3.3 constant_dynamic-update-slice_fusion.6
  143.4 1.6 dynamic-slice_bitcast_fusion.3
  148.9 39.8 %while.49 = (s32[]{:T(128)}, bf16[4,128,5,128]{1,3,2,0:T(8,128)(2,1)}, f32[4,640,128]{2,1,0:T(8,128)}, f32[4,640,128]{2,1,0:T(8,128)}, s32[4]{0:T(128)S(1)}, /*i...) while((s32[]{:T(128)}, ...), condition=%wide.region_5.5_spmd, body=%wide.region_1.4_spmd.sunk | while | flops 633733120 | bytes 16154433 | solution.py:96
  151.2 1.6 exponential_reduce_fusion.2
  155.9 1.9 fusion.97
  165.8 1.9 fusion.97
  171.1 1.6 exponential_reduce_fusion.2
  175.8 1.9 fusion.97
  181.1 1.6 exponential_reduce_fusion.2
  185.7 1.9 fusion.97
  188.8 2.2 copy.79
  196.3 3.3 constant_dynamic-update-slice_fusion.6
  199.6 1.9 slice.41
  202.1 2.7 pad_maximum_fusion.2
  204.8 4.9 %reshape.83 = f32[8,131072]{1,0:T(8,128)} reshape(f32[2,4,2,128,512]{4,3,2,1,0:T(8,128)} %pad_maximum_fusion.2) | data formatting | bytes 8388608 | tf_op jit(solution)/shard_map/reshape | solution.py:121
  209.7 10.3 %convolution_convert_fusion = bf16[32,2,128,512]{3,0,2,1:T(8,128)(2,1)} fusion(f32[2,128,512,8]{2,3,1,0:T(8,128)} %bitcast.190, s32[8]{0:T(128)S(1)} %copy-done.11), kind=kOutput, calls=%fused_computation.62 | convolution fusion | flops 406847744 | bytes 12582944 | tf_op jit(solution)/shard_map/dot_general | solution.py:124
  220.0 11.4 %copy.51 = bf16[32,2,128,512]{3,2,1,0:T(8,128)(2,1)} copy(bf16[32,2,128,512]{3,0,2,1:T(8,128)(2,1)} %convolution_convert_fusion) | data formatting | bytes 16777216 | tf_op jit(solution)/shard_map/convert_element_type | solution.py:128
  233.4 97.9 %reduce-scatter.2.cloned.1.call-done = bf16[1,2,128,512]{3,2,1,0:T(8,128)(2,1)} async-done(((bf16[32,2,128,512]{3,2,1,0:T(8,128)(2,1)}), bf16[1,2,128,512]{3,2,1,0:T(8,128)(2,1)}) %reduce-scatter.2.cloned.1.call-update) | async-done | bytes 262160 | tf_op jit(solution)/shard_map/reduce_scatter | solution.py:127
  (190 shorter events, 73.1 us)
Async XLA Ops:
  7.2 2.9 copy-start
  7.2 64.1 %all-gather.2.cloned.1.call-start = ((), (), s32[]{:S(2)}) async-start(), calls=%async_computation.1 | async-start | bytes 8650752 | tf_op jit(solution)/shard_map/all_gather | solution.py:53
  7.9 323.3 %reduce-scatter.2.cloned.1.call-start = ((), (), s32[]{:S(2)}) async-start(), calls=%async_computation.2 | async-start | bytes 8650752 | tf_op jit(solution)/shard_map/reduce_scatter | solution.py:127
  78.7 7.1 %copy-start.4 = (bf16[2,4,2,128,512]{4,3,2,1,0:T(8,128)(2,1)}, bf16[2,4,2,128,512]{4,3,2,1,0:T(8,128)(2,1)S(1)}, u32[]{:S(2)}) copy-start(bf16[2,4,2,128,512]{4,3,2,1,0:T(8,128)(2,1)S(1)} %get-tuple-element.680) | copy-start | bytes 6291460 | tf_op jit(solution)/shard_map/while
  82.0 3.7 %copy-start.8 = (bf16[256,2560]{1,0:T(8,128)(2,1)S(1)}, bf16[256,2560]{1,0:T(8,128)(2,1)}, u32[]{:S(2)}) copy-start(bf16[256,2560]{1,0:T(8,128)(2,1)} %get-tuple-element.678) | copy-start | bytes 3932164 | tf_op jit(solution)/shard_map/while
  85.8 0.9 copy-start.7
  86.0 2.5 copy-start.10
  92.4 1.1 copy-start.2
  102.3 1.1 copy-start.2
  112.3 1.1 copy-start.2
  122.2 1.1 copy-start.2
  130.5 1.1 copy-start.6
  131.8 1.6 copy-start.3
  135.8 3.3 copy-start.5
  139.1 7.1 %copy-start.4 = (bf16[2,4,2,128,512]{4,3,2,1,0:T(8,128)(2,1)}, bf16[2,4,2,128,512]{4,3,2,1,0:T(8,128)(2,1)S(1)}, u32[]{:S(2)}) copy-start(bf16[2,4,2,128,512]{4,3,2,1,0:T(8,128)(2,1)S(1)} %get-tuple-element.680) | copy-start | bytes 6291460 | tf_op jit(solution)/shard_map/while
  142.4 3.7 %copy-start.8 = (bf16[256,2560]{1,0:T(8,128)(2,1)S(1)}, bf16[256,2560]{1,0:T(8,128)(2,1)}, u32[]{:S(2)}) copy-start(bf16[256,2560]{1,0:T(8,128)(2,1)} %get-tuple-element.678) | copy-start | bytes 3932164 | tf_op jit(solution)/shard_map/while
  146.2 0.9 copy-start.7
  146.4 2.5 copy-start.10
  152.8 1.1 copy-start.2
  162.8 1.1 copy-start.2
  172.7 1.1 copy-start.2
  182.7 1.1 copy-start.2
  190.9 1.1 copy-start.6
  192.3 1.6 copy-start.3
  196.3 3.3 copy-start.5
  199.6 2.4 copy-start.9
  204.8 4.9 %copy-start.11 = (s32[8]{0:T(128)S(1)}, s32[8]{0:T(128)}, u32[]{:S(2)}) copy-start(s32[8]{0:T(128)} %eq.16) | copy-start | bytes 100
  231.4 99.9 %copy-start.1 = (s32[32]{0:T(128)S(1)}, s32[32]{0:T(128)}, u32[]{:S(2)}) copy-start(s32[32]{0:T(128)} %param.15) | copy-start | bytes 388
Sparse Core Ops, SparseCore 0:
  10.5 60.7 all-gather.1
  231.5 99.7 reduce-scatter.1
where the time goes:
time: 340 us; the launch traced here: 338 us
  waiting for transfers between devices  158 us (46%)
  local copies, waits for them, and re-layouts  72.5 us (21%)
  matrix products  63 us (19%)
  loops' own time  16.3 us (5%)
  other arithmetic  14.6 us (4%)
  between operations  14.1 us (4%)
    reduce_scatter x1, waiting for transfers between devices, body(): lax.psum_scatter(block_sum.astype(jnp.bfloat16), 'comp', scatter_dimensio...  97.9 us
    all_gather x1, waiting for transfers between devices, body(): portion = lax.all_gather(node_kv, 'comp', axis=0, tiled=True)  59 us
    dot_general x8, matrix products, head_block(): jnp.einsum('gij,jd->igd', score_low, key_block, preferred_element_type=jn...  15.3 us
    sub x8, matrix products, head_block(): weights = jnp.exp(scores - top_score)  13 us
    convert_element_type x1, local copies, waits for them, and re-layouts, body(): block_sum.astype(jnp.bfloat16)  11.4 us
    while x44, local copies, waits for them, and re-layouts  10.7 us
    another operation x2, loops' own time, completion(): lax.map(head_share, jnp.arange(KV_HEADS))  10.7 us
    dot_general x1, matrix products, body(): jnp.dot(one_hot, node_terms, precision=lax.Precision.HIGHEST)  10.3 us
  transfers between devices with their start and end apart: 2, of which 2 were waited for; matrix products, arithmetic and copies ran while one was open for 2% of the time, Pallas kernels for 0%

commit v1 on v0

v1 whole, which is shorter than its diff:
```python
import functools
import math

import jax
import jax.numpy as jnp
from jax import lax
from jax.experimental import pallas as pl
from jax.experimental.pallas import tpu as pltpu
from jax.sharding import Mesh
from jax.sharding import PartitionSpec as P

QUERY_HEADS = 20
KV_HEADS = 4
HEAD_SIZE = 128
TILE_SLOTS = 128
DEPTH = 4
QUERY_LENGTH = 128
GROUP_SHARE = QUERY_HEADS // KV_HEADS
KEY_ROWS = DEPTH * TILE_SLOTS + QUERY_LENGTH


def attention_kernel(lens_ref, q_ref, do_ref, k_ref, v_ref, dq_ref, dk_ref, dv_ref):
    c = pl.program_id(0)
    factor = 1.0 / math.sqrt(HEAD_SIZE)
    key_block = k_ref[...]
    value_block = v_ref[...]
    col = lax.broadcasted_iota(jnp.int32, (QUERY_LENGTH, KEY_ROWS), 1)
    row = lax.broadcasted_iota(jnp.int32, (QUERY_LENGTH, KEY_ROWS), 0)
    level = col // TILE_SLOTS
    slot = col % TILE_SLOTS
    limit = jnp.where(
        level == 0,
        lens_ref[c, 0],
        jnp.where(level == 1, lens_ref[c, 1], jnp.where(level == 2, lens_ref[c, 2], lens_ref[c, 3])),
    )
    visible = ((level < DEPTH) & (slot < limit)) | (
        (level >= DEPTH) & ((col - DEPTH * TILE_SLOTS) <= row)
    )
    dk_acc = jnp.zeros((KEY_ROWS, HEAD_SIZE), jnp.float32)
    dv_acc = jnp.zeros((KEY_ROWS, HEAD_SIZE), jnp.float32)
    nt = (((1,), (1,)), ((), ()))
    tn = (((0,), (0,)), ((), ()))
    for g in range(GROUP_SHARE):
        cols = slice(g * HEAD_SIZE, (g + 1) * HEAD_SIZE)
        query_g = q_ref[:, cols]
        cot_g = do_ref[:, cols]
        scores = lax.dot_general(query_g, key_block, nt, preferred_element_type=jnp.float32) * factor
        scores = jnp.where(visible, scores, -jnp.inf)
        top = jnp.max(scores, axis=-1, keepdims=True)
        weights = jnp.exp(scores - top)
        probs = weights / jnp.sum(weights, axis=-1, keepdims=True)
        probs_low = probs.astype(jnp.bfloat16)
        outputs = jnp.dot(probs_low, value_block, preferred_element_type=jnp.float32)
        centre = jnp.sum(cot_g.astype(jnp.float32) * outputs, axis=-1, keepdims=True)
        prob_grads = lax.dot_general(cot_g, value_block, nt, preferred_element_type=jnp.float32)
        score_low = (probs * (prob_grads - centre)).astype(jnp.bfloat16)
        dq = jnp.dot(score_low, key_block, preferred_element_type=jnp.float32) * factor
        dq_ref[:, cols] = dq.astype(jnp.bfloat16)
        dk_acc = dk_acc + lax.dot_general(score_low, query_g, tn, preferred_element_type=jnp.float32)
        dv_acc = dv_acc + lax.dot_general(probs_low, cot_g, tn, preferred_element_type=jnp.float32)
    dk_ref[...] = dk_acc * factor
    dv_ref[...] = dv_acc


def attention(lens, queries, cotangent, keys, values):
    members = keys.shape[0]
    width = GROUP_SHARE * HEAD_SIZE
    row_block = pl.BlockSpec((QUERY_LENGTH, width), lambda c, h, lens: (c, h))
    key_block = pl.BlockSpec((None, KEY_ROWS, HEAD_SIZE), lambda c, h, lens: (c, 0, h))
    grid_spec = pltpu.PrefetchScalarGridSpec(
        num_scalar_prefetch=1,
        grid=(members, KV_HEADS),
        in_specs=[row_block, row_block, key_block, key_block],
        out_specs=[row_block, key_block, key_block],
    )
    return pl.pallas_call(
        attention_kernel,
        grid_spec=grid_spec,
        out_shape=[
            jax.ShapeDtypeStruct(queries.shape, jnp.bfloat16),
            jax.ShapeDtypeStruct(keys.shape, jnp.float32),
            jax.ShapeDtypeStruct(keys.shape, jnp.float32),
        ],
    )(lens, queries, cotangent, keys, values)


def body(queries, suffix_key_value, output_gradient, node_kv, paths, tile_lens):
    members = paths.shape[0]
    span_width = node_kv.shape[-1]
    cores = lax.psum(1, "core")
    chips = lax.psum(1, "chip")
    node_count = cores * chips
    trie_node_rows = DEPTH * TILE_SLOTS
    portion = lax.all_gather(node_kv, "chip", axis=0, tiled=True)
    portion = lax.all_gather(portion, "core", axis=0, tiled=True)
    node_ids = jnp.clip(paths, 0, node_count - 1)
    where_held = (node_ids % cores) * chips + node_ids // cores
    path_tiles = jnp.take(portion, where_held.reshape(-1), axis=0).reshape(
        (members, DEPTH) + node_kv.shape[1:]
    )
    suffix_rows = suffix_key_value.reshape(2, members, QUERY_LENGTH, span_width)
    keys = jnp.concatenate(
        [path_tiles[:, :, 0].reshape(members, trie_node_rows, span_width), suffix_rows[0]], axis=1
    )
    values = jnp.concatenate(
        [path_tiles[:, :, 1].reshape(members, trie_node_rows, span_width), suffix_rows[1]], axis=1
    )
    lens = jnp.take(tile_lens, node_ids).astype(jnp.int32)
    query_out, key_gradient, value_gradient = attention(
        lens, queries, output_gradient, keys, values
    )
    suffix_out = jnp.stack(
        [key_gradient[:, trie_node_rows:], value_gradient[:, trie_node_rows:]], axis=0
    ).reshape(2, members * QUERY_LENGTH, span_width).astype(jnp.bfloat16)
    terms = jnp.stack(
        [
            key_gradient[:, :trie_node_rows].reshape(members, DEPTH, TILE_SLOTS, span_width),
            value_gradient[:, :trie_node_rows].reshape(members, DEPTH, TILE_SLOTS, span_width),
        ],
        axis=2,
    )
    block_sum = jnp.zeros((node_count,) + node_kv.shape[1:], jnp.bfloat16)
    merged = [terms[0]]
    for c in range(1, members):
        same = (node_ids[c] == node_ids[0])[:, None, None, None]
        merged[0] = merged[0] + jnp.where(same, terms[c], 0.0)
    merged[0] = merged[0].astype(jnp.bfloat16)
    for c in range(1, members):
        same = (node_ids[c] == node_ids[0])[:, None, None, None]
        merged.append(jnp.where(same, merged[0].astype(jnp.float32), terms[c]).astype(jnp.bfloat16))
    for c in range(members):
        for level in range(DEPTH):
            block_sum = lax.dynamic_update_slice(
                block_sum, merged[c][level][None], (where_held[c, level], 0, 0, 0)
            )
    partial = lax.psum_scatter(block_sum, "core", scatter_dimension=0, tiled=True)
    node_out = lax.psum_scatter(partial, "chip", scatter_dimension=0, tiled=True)
    return (query_out, suffix_out, node_out)


def solution(mesh):
    chips = mesh.shape["comp"] // 2
    devices = mesh.devices.reshape(chips, 2, mesh.shape["prompt"])
    split_mesh = Mesh(devices, ("chip", "core", "prompt"))
    rows = ("prompt", "chip", "core")
    in_specs = (
        P(rows, None),
        P(None, rows, None),
        P(rows, None),
        P(rows, None, None, None),
        P(rows, None),
        P("prompt"),
    )
    out_specs = (
        P(rows, None),
        P(None, rows, None),
        P(rows, None, None, None),
    )
    return jax.shard_map(
        body, mesh=split_mesh, in_specs=in_specs, out_specs=out_specs, check_vma=False
    )
```

time: 340 us -> 269 us (0.79)
  matrix products: 63 us -> 0 us
  local copies, waits for them, and re-layouts: 72.5 us -> 19.5 us
  Pallas kernels: 0 us -> 34.4 us
  waiting for transfers between devices: 158 us -> 181 us
  loops' own time: 16.3 us -> 0 us
  between operations: 14.1 us -> 29.1 us
  other arithmetic: 14.6 us -> 4.12 us
    unnamed x2 -> x5, waiting for transfers between devices: 0.7 us -> 87.2 us
    reduce_scatter x1, waiting for transfers between devices: 97.9 us -> 23.3 us  [body(): lax.psum_scatter(block_sum, 'core', scatter_dimension=0, tiled=True)]
    dot_general x41 -> x0, matrix products: 50 us -> none  [the longest x8 15.3 us: head_block(): jnp.einsum('gij,jd->igd', score_low, key_block, preferred_element_type=jn...]
    pallas_call x0 -> x1, Pallas kernels: none -> 34.4 us  [attention(): pl.pallas_call(attention_kernel, grid_spec=grid_spec, out_shape=[jax.Shap...]
    another operation x3 -> x0, loops' own time: 16.3 us -> none  [the longest x2 10.7 us: completion(): lax.map(head_share, jnp.arange(KV_HEADS))]
    sub x8 -> x0, matrix products: 13 us -> none  [head_block(): weights = jnp.exp(scores - top_score)]
    all_gather x1 -> x2, waiting for transfers between devices: 59 us -> 71.1 us  [the longest x1 61.9 us: body(): portion = lax.all_gather(node_kv, 'chip', axis=0, tiled=True)]
    dynamic_slice x38 -> x0, local copies, waits for them, and re-layouts: 11.4 us -> none  [the longest x8 4.66 us: completion(): lax.map(head_share, jnp.arange(KV_HEADS))]
  transfers between devices with their start and end apart: 2 -> 4, of which waited for: 2 -> 4; matrix products, arithmetic and copies ran while one was open for 2% -> 2% of each run, Pallas kernels for 0% -> 0%
where the time goes in v1:
time: 269 us
  waiting for transfers between devices  181 us (67%)
  Pallas kernels  34.4 us (13%)
  between operations  29.1 us (11%)
  local copies, waits for them, and re-layouts  19.5 us (7%)
  other arithmetic  4.12 us (2%)
    unnamed x5, waiting for transfers between devices  87.2 us
    all_gather x1, waiting for transfers between devices, body(): portion = lax.all_gather(node_kv, 'chip', axis=0, tiled=True)  61.9 us
    pallas_call x1, Pallas kernels, attention(): pl.pallas_call(attention_kernel, grid_spec=grid_spec, out_shape=[jax.Shap...  34.4 us
    reduce_scatter x1, waiting for transfers between devices, body(): lax.psum_scatter(block_sum, 'core', scatter_dimension=0, tiled=True)  23.3 us
    all_gather x1, waiting for transfers between devices, body(): portion = lax.all_gather(portion, 'core', axis=0, tiled=True)  9.2 us
    dynamic_update_slice x8, local copies, waits for them, and re-layouts, body(): lax.dynamic_update_slice(block_sum, merged[c][level][None], (where_held[c...  5.76 us
  transfers between devices with their start and end apart: 4, of which 4 were waited for; matrix products, arithmetic and copies ran while one was open for 2% of the time, Pallas kernels for 0%

profile of v1, /device:TPU:2, one launch (start us, length us, event | category | flops | bytes accessed | tf_op | source)
XLA Modules:
  0.0 268.8 jit_solution(8277638069869572377)
XLA Ops:
  7.2 0.7 all-gather.3.cloned.1.call-update
  8.0 61.9 %all-gather.3.cloned.1.call-done = bf16[16,2,128,512]{3,2,1,0:T(8,128)(2,1)} async-done(((bf16[1,2,128,512]{3,2,1,0:T(8,128)(2,1)}), bf16[16,2,128,512]{3,2,1,0:T(8,128)(2,1)}) %all-gather.3.cloned.1.call-update) | async-done | bytes 4194320 | tf_op jit(solution)/shard_map/all_gather | solution.py:94
  69.9 0.1 reshape.73
  70.0 0.7 fusion.12
  80.8 0.1 reshape.76
  80.9 0.6 gather_fusion
  81.6 0.1 reshape.75
  86.8 0.6 broadcast_clamp_fusion
  87.4 9.2 %all-gather.5.cloned.1.call-done = bf16[32,2,128,512]{3,2,1,0:T(8,128)(2,1)} async-done(((bf16[16,2,128,512]{3,2,1,0:T(8,128)(2,1)}), bf16[32,2,128,512]{3,2,1,0:T(8,128)(2,1)}) %all-gather.5.cloned.1.call-update) | async-done | bytes 8388624 | tf_op jit(solution)/shard_map/all_gather | solution.py:95
  96.6 4.1 %gather_fusion.1 = bf16[8,2,128,512]{3,2,1,0:T(8,128)(2,1)S(1)} fusion(bf16[32,2,128,512]{3,2,1,0:T(8,128)(2,1)} %all-gather.5.cloned.1.call-done, s32[1024]{0:T(1024)S(1)} %pad_clamp_fusion), kind=kCustom, calls=%fused_computation.1 | custom fusion | bytes 4194336 | tf_op jit(solution)/shard_map/jit(_take)/gather | solution.py:98
  100.7 0.3 copy_select_fusion
  100.9 0.2 fusion.10
  101.1 1.7 pad_maximum_fusion.1
  102.8 34.4 %shard_map.85 = (bf16[256,2560]{1,0:T(8,128)(2,1)}, f32[2,640,512]{2,1,0:T(8,128)}, f32[2,640,512]{2,1,0:T(8,128)}) custom-call(s32[2,4]{1,0:T(2,128)} %get-tuple-element.26.lens_ref, bf16[256,2560]{1,0:T(8,128)(2,1)} %q_ref.1, bf16[256,2560]{1,0:T(8,128)(2,1)} %do_ref.1, bf16[2,640,512]{2,1,0:T(8,128)(2,1)} %get-tuple-element.27.k_ref, ...), custom_call_target="tpu_custom_call" | custom-call | tf_op jit(solution)/shard_map/pallas_call | solution.py:76
  137.2 1.9 slice.97
  139.1 0.5 copy-done.1
  139.6 0.2 slice.98
  139.7 0.7 select_convert_fusion
  140.4 4.3 %broadcast_in_dim.40 = bf16[32,2,128,512]{3,2,1,0:T(8,128)(2,1)} broadcast(bf16[]{:T(256)} %constant.61.clone.1), dimensions={} | broadcast | bytes 8388610 | tf_op jit(solution)/shard_map/broadcast_in_dim | solution.py:122
  144.7 0.7 slice_dynamic-update-slice_fusion.7
  145.4 0.7 slice_dynamic-update-slice_fusion.6
  146.1 0.7 slice_dynamic-update-slice_fusion.5
  146.9 0.7 slice_dynamic-update-slice_fusion.4
  147.6 0.7 slice_dynamic-update-slice_fusion.3
  148.3 0.7 slice_dynamic-update-slice_fusion.2
  149.0 0.7 slice_dynamic-update-slice_fusion.1
  149.7 0.7 slice_dynamic-update-slice_fusion
  150.5 0.0 reduce-scatter.7.cloned.1.call-start
  150.5 23.3 %reduce-scatter.5.cloned.1.call-done = bf16[16,2,128,512]{3,2,1,0:T(8,128)(2,1)} async-done(((bf16[32,2,128,512]{3,2,1,0:T(8,128)(2,1)}), bf16[16,2,128,512]{3,2,1,0:T(8,128)(2,1)}) %reduce-scatter.5.cloned.1.call-update) | async-done | bytes 4194320 | tf_op jit(solution)/shard_map/reduce_scatter | solution.py:136
  173.8 1.1 slice.162
  175.0 0.8 pad_maximum_fusion.3
  175.8 86.4 %reduce-scatter.7.cloned.1.call-done = bf16[1,2,128,512]{3,2,1,0:T(8,128)(2,1)} async-done(((bf16[16,2,128,512]{3,2,1,0:T(8,128)(2,1)}), bf16[1,2,128,512]{3,2,1,0:T(8,128)(2,1)}) %reduce-scatter.7.cloned.1.call-update) | async-done | bytes 262160
  (21 shorter events, 0.3 us)
Async XLA Ops:
  7.2 73.7 %copy-start = (s32[32]{0:T(128)S(1)}, s32[32]{0:T(128)}, u32[]{:S(2)}) copy-start(s32[32]{0:T(128)} %param.11) | copy-start | bytes 388
  7.2 62.7 %copy-start.3 = (s32[2,4]{1,0:T(2,128)S(1)}, s32[2,4]{1,0:T(2,128)}, u32[]{:S(2)}) copy-start(s32[2,4]{1,0:T(2,128)} %param.10) | copy-start | bytes 100
  7.2 62.6 %all-gather.3.cloned.1.call-start = ((), (), s32[]{:S(2)}) async-start(), calls=%async_computation.2 | async-start | bytes 4456448 | tf_op jit(solution)/shard_map/all_gather | solution.py:94
  7.9 88.7 %all-gather.5.cloned.1.call-start = ((), (), s32[]{:S(2)}) async-start(), calls=%async_computation.3 | async-start | bytes 12582912 | tf_op jit(solution)/shard_map/all_gather | solution.py:95
  69.8 17.5 %copy-start.2 = (bf16[2,256,512]{2,1,0:T(8,128)(2,1)S(1)}, bf16[2,256,512]{2,1,0:T(8,128)(2,1)}, u32[]{:S(2)}) copy-start(bf16[2,256,512]{2,1,0:T(8,128)(2,1)} %param.7) | copy-start | bytes 1572868
  69.9 104.0 %reduce-scatter.5.cloned.1.call-start = ((), (), s32[]{:S(2)}) async-start(), calls=%async_computation.4 | async-start | bytes 12582912 | tf_op jit(solution)/shard_map/reduce_scatter | solution.py:136
  137.2 2.4 copy-start.1
  150.5 111.7 %reduce-scatter.7.cloned.1.call-start = ((), (), s32[]{:S(2)}) async-start(), calls=%async_computation.5 | async-start | bytes 4456448
Sparse Core Ops, SparseCore 0:
  10.4 59.3 all-gather.2
  71.6 24.9 all-gather.4
  150.6 23.1 reduce-scatter.4
  177.9 84.3 reduce-scatter.6

commit v2 on v1

v2 whole, which is shorter than its diff:
```python
import math

import jax
import jax.numpy as jnp
from jax import lax
from jax.experimental import pallas as pl
from jax.experimental.pallas import tpu as pltpu
from jax.sharding import PartitionSpec as P

QUERY_HEADS = 20
KV_HEADS = 4
HEAD_SIZE = 128
TILE_SLOTS = 128
DEPTH = 4
QUERY_LENGTH = 128
GROUP_SHARE = QUERY_HEADS // KV_HEADS
NODE_ROWS = DEPTH * TILE_SLOTS
KEY_ROWS = NODE_ROWS + QUERY_LENGTH
STACK_ROWS = GROUP_SHARE * QUERY_LENGTH


def attention_kernel(ids_ref, lens_ref, q_ref, do_ref, *refs):
    node_k = refs[0:DEPTH]
    node_v = refs[DEPTH : 2 * DEPTH]
    own_k, own_v, dq_ref, dk_ref, dv_ref = refs[2 * DEPTH :]
    c = pl.program_id(1)
    factor = 1.0 / math.sqrt(HEAD_SIZE)
    key_block = jnp.concatenate([r[...] for r in node_k] + [own_k[...]], axis=0)
    value_block = jnp.concatenate([r[...] for r in node_v] + [own_v[...]], axis=0)
    heads = [slice(g * HEAD_SIZE, (g + 1) * HEAD_SIZE) for g in range(GROUP_SHARE)]
    query_rows = jnp.concatenate([q_ref[:, cols] for cols in heads], axis=0)
    cot_rows = jnp.concatenate([do_ref[:, cols] for cols in heads], axis=0)
    col = lax.broadcasted_iota(jnp.int32, (STACK_ROWS, KEY_ROWS), 1)
    row = lax.broadcasted_iota(jnp.int32, (STACK_ROWS, KEY_ROWS), 0) % QUERY_LENGTH
    level = col // TILE_SLOTS
    slot = col % TILE_SLOTS
    limit = jnp.where(
        level == 0,
        lens_ref[c, 0],
        jnp.where(level == 1, lens_ref[c, 1], jnp.where(level == 2, lens_ref[c, 2], lens_ref[c, 3])),
    )
    visible = ((level < DEPTH) & (slot < limit)) | ((level >= DEPTH) & ((col - NODE_ROWS) <= row))
    nt = (((1,), (1,)), ((), ()))
    tn = (((0,), (0,)), ((), ()))
    scores = lax.dot_general(query_rows, key_block, nt, preferred_element_type=jnp.float32) * factor
    scores = jnp.where(visible, scores, -jnp.inf)
    top = jnp.max(scores, axis=-1, keepdims=True)
    weights = jnp.exp(scores - top)
    probs = weights / jnp.sum(weights, axis=-1, keepdims=True)
    probs_low = probs.astype(jnp.bfloat16)
    outputs = jnp.dot(probs_low, value_block, preferred_element_type=jnp.float32)
    centre = jnp.sum(cot_rows.astype(jnp.float32) * outputs, axis=-1, keepdims=True)
    prob_grads = lax.dot_general(cot_rows, value_block, nt, preferred_element_type=jnp.float32)
    score_low = (probs * (prob_grads - centre)).astype(jnp.bfloat16)
    dq = (jnp.dot(score_low, key_block, preferred_element_type=jnp.float32) * factor).astype(jnp.bfloat16)
    for g, cols in enumerate(heads):
        dq_ref[:, cols] = dq[g * QUERY_LENGTH : (g + 1) * QUERY_LENGTH]
    dk = lax.dot_general(score_low, query_rows, tn, preferred_element_type=jnp.float32) * factor
    dv = lax.dot_general(probs_low, cot_rows, tn, preferred_element_type=jnp.float32)

    @pl.when(c == 0)
    def _():
        dk_ref[0] = dk
        dv_ref[0] = dv

    @pl.when(c == 1)
    def _():
        for level_at in range(DEPTH):
            rows = slice(level_at * TILE_SLOTS, (level_at + 1) * TILE_SLOTS)
            same = ids_ref[0, level_at] == ids_ref[1, level_at]
            for out_ref, term in ((dk_ref, dk), (dv_ref, dv)):
                before = out_ref[0, rows, :]
                here = term[rows]
                summed = before + here
                out_ref[0, rows, :] = jnp.where(same, summed, before)
                out_ref[1, rows, :] = jnp.where(same, summed, here)
        dk_ref[1, NODE_ROWS:, :] = dk[NODE_ROWS:]
        dv_ref[1, NODE_ROWS:, :] = dv[NODE_ROWS:]


def attention(ids, lens, queries, cotangent, portion, suffix_key_value):
    members = ids.shape[0]
    width = GROUP_SHARE * HEAD_SIZE
    row_block = pl.BlockSpec((QUERY_LENGTH, width), lambda h, c, ids, lens: (c, h))

    def node_block(level_at, half):
        return pl.BlockSpec(
            (None, None, TILE_SLOTS, HEAD_SIZE),
            lambda h, c, ids, lens: (ids[c, level_at], half, 0, h),
        )

    def own_block(half):
        return pl.BlockSpec((None, QUERY_LENGTH, HEAD_SIZE), lambda h, c, ids, lens: (half, c, h))

    grad_block = pl.BlockSpec((members, KEY_ROWS, HEAD_SIZE), lambda h, c, ids, lens: (0, 0, h))
    in_specs = (
        [row_block, row_block]
        + [node_block(level_at, 0) for level_at in range(DEPTH)]
        + [node_block(level_at, 1) for level_at in range(DEPTH)]
        + [own_block(0), own_block(1)]
    )
    grid_spec = pltpu.PrefetchScalarGridSpec(
        num_scalar_prefetch=2,
        grid=(KV_HEADS, members),
        in_specs=in_specs,
        out_specs=[row_block, grad_block, grad_block],
    )
    grad_shape = jax.ShapeDtypeStruct((members, KEY_ROWS, KV_HEADS * HEAD_SIZE), jnp.float32)
    return pl.pallas_call(
        attention_kernel,
        grid_spec=grid_spec,
        out_shape=[jax.ShapeDtypeStruct(queries.shape, jnp.bfloat16), grad_shape, grad_shape],
        compiler_params=pltpu.CompilerParams(vmem_limit_bytes=48 * 1024 * 1024),
    )(ids, lens, queries, cotangent, *([portion] * (2 * DEPTH)), suffix_key_value, suffix_key_value)


def body(queries, suffix_key_value, output_gradient, node_kv, paths, tile_lens):
    members = paths.shape[0]
    span_width = node_kv.shape[-1]
    portion = lax.all_gather(node_kv, "comp", axis=0, tiled=True)
    node_count = portion.shape[0]
    ids = jnp.clip(paths, 0, node_count - 1).astype(jnp.int32)
    lens = jnp.take(tile_lens, ids).astype(jnp.int32)
    query_out, key_gradient, value_gradient = attention(
        ids, lens, queries, output_gradient, portion, suffix_key_value
    )
    suffix_out = jnp.stack(
        [key_gradient[:, NODE_ROWS:], value_gradient[:, NODE_ROWS:]], axis=0
    ).reshape(2, members * QUERY_LENGTH, span_width).astype(jnp.bfloat16)
    slots = ids.reshape(members * DEPTH)
    hits = slots[None, :] == jnp.arange(node_count, dtype=jnp.int32)[:, None]
    slot_of = jnp.argmax(hits, axis=1)
    held = jnp.any(hits, axis=1)[:, None, None, None]
    slot_grads = jnp.stack(
        [
            key_gradient[:, :NODE_ROWS].reshape(members * DEPTH, TILE_SLOTS, span_width),
            value_gradient[:, :NODE_ROWS].reshape(members * DEPTH, TILE_SLOTS, span_width),
        ],
        axis=1,
    )
    block_sum = jnp.where(held, jnp.take(slot_grads, slot_of, axis=0), 0.0).astype(jnp.bfloat16)
    node_out = lax.psum_scatter(block_sum, "comp", scatter_dimension=0, tiled=True)
    return (query_out, suffix_out, node_out)


def solution(mesh):
    rows = ("prompt", "comp")
    in_specs = (
        P(rows, None),
        P(None, rows, None),
        P(rows, None),
        P(rows, None, None, None),
        P(rows, None),
        P("prompt"),
    )
    out_specs = (
        P(rows, None),
        P(None, rows, None),
        P(rows, None, None, None),
    )
    return jax.shard_map(body, mesh=mesh, in_specs=in_specs, out_specs=out_specs, check_vma=False)
```

time: 269 us -> 225 us (0.84)
  waiting for transfers between devices: 181 us -> 159 us
  between operations: 29.1 us -> 14.1 us
  Pallas kernels: 34.4 us -> 22.2 us
  other arithmetic: 4.12 us -> 15.5 us
  local copies, waits for them, and re-layouts: 19.5 us -> 13.9 us
    unnamed x5 -> x2, waiting for transfers between devices: 87.2 us -> 0.7 us
    reduce_scatter x1, waiting for transfers between devices: 23.3 us -> 97.9 us  [body(): lax.psum_scatter(block_sum, 'comp', scatter_dimension=0, tiled=True)]
    pallas_call x1, Pallas kernels: 34.4 us -> 22.2 us  [attention(): pl.pallas_call(attention_kernel, grid_spec=grid_spec, out_shape=[jax.Shap...]
    all_gather x2 -> x1, waiting for transfers between devices: 71.1 us -> 60.4 us  [body(): portion = lax.all_gather(node_kv, 'comp', axis=0, tiled=True)]
    convert_element_type x1, other arithmetic: 0.7 us -> 11 us  [body(): jnp.where(held, jnp.take(slot_grads, slot_of, axis=0), 0.0)]
    dynamic_update_slice x8 -> x0, local copies, waits for them, and re-layouts: 5.76 us -> none  [body(): lax.dynamic_update_slice(block_sum, merged[c][level][None], (where_held[c...]
    broadcast_in_dim x2 -> x1, local copies, waits for them, and re-layouts: 4.33 us -> 0.08 us  [body(): lens = jnp.take(tile_lens, ids).astype(jnp.int32)]
    unnamed x8, local copies, waits for them, and re-layouts: 0.47 us -> 3.68 us
  transfers between devices with their start and end apart: 4 -> 2, of which waited for: 4 -> 2; matrix products, arithmetic and copies ran while one was open for 2% -> 2% of each run, Pallas kernels for 0% -> 0%
where the time goes in v2:
time: 225 us
  waiting for transfers between devices  159 us (71%)
  Pallas kernels  22.2 us (10%)
  other arithmetic  15.5 us (7%)
  between operations  14.1 us (6%)
  local copies, waits for them, and re-layouts  13.9 us (6%)
    reduce_scatter x1, waiting for transfers between devices, body(): lax.psum_scatter(block_sum, 'comp', scatter_dimension=0, tiled=True)  97.9 us
    all_gather x1, waiting for transfers between devices, body(): portion = lax.all_gather(node_kv, 'comp', axis=0, tiled=True)  60.4 us
    pallas_call x1, Pallas kernels, attention(): pl.pallas_call(attention_kernel, grid_spec=grid_spec, out_shape=[jax.Shap...  22.2 us
    convert_element_type x1, other arithmetic, body(): jnp.where(held, jnp.take(slot_grads, slot_of, axis=0), 0.0)  11 us
    gather x1, local copies, waits for them, and re-layouts, body(): jnp.take(slot_grads, slot_of, axis=0)  6.38 us
  transfers between devices with their start and end apart: 2, of which 2 were waited for; matrix products, arithmetic and copies ran while one was open for 2% of the time, Pallas kernels for 0%

profile of v2, /device:TPU:2, one launch (start us, length us, event | category | flops | bytes accessed | tf_op | source)
XLA Modules:
  0.0 224.7 jit_solution(15906389187681363671)
XLA Ops:
  7.2 0.0 copy-start
  7.2 0.0 all-gather.2.cloned.1.call-start
  7.2 0.7 all-gather.2.cloned.1.call-update
  7.9 0.0 reduce-scatter.2.cloned.1.call-start
  8.0 0.7 compare_select_fusion
  8.6 0.1 reshape.27
  8.7 0.0 copy-done
  8.7 0.6 gather_fusion
  9.4 0.1 reshape.26
  9.5 0.7 and_select_fusion
  10.2 0.1 eq.17
  10.2 0.6 iota_reduce_fusion
  10.9 0.1 fusion
  11.0 60.4 %all-gather.2.cloned.1.call-done.refs_0_.refs_1_.refs_2_.refs_3_.refs_4_.refs_5_.refs_6_.refs_7_ = bf16[32,2,128,512]{3,2,1,0:T(8,128)(2,1)} async-done(((bf16[1,2,128,512]{3,2,1,0:T(8,128)(2,1)}), bf16[32,2,128,512]{3,2,1,0:T(8,128)(2,1)}) %all-gather.2.cloned.1.call-update) | async-done | bytes 8388624 | tf_op jit(solution)/shard_map/all_gather | solution.py:120
  71.3 0.0 copy-start.1
  71.3 1.0 copy-done.1
  72.3 0.0 copy-start.2
  72.3 1.3 copy-done.2
  73.7 0.0 copy-start.3
  73.7 1.3 copy-done.3
  75.0 22.2 %shard_map.85 = (bf16[256,2560]{1,0:T(8,128)(2,1)}, f32[2,640,512]{2,1,0:T(8,128)S(1)}, f32[2,640,512]{2,1,0:T(8,128)}) custom-call(s32[2,4]{1,0:T(2,128)S(1)} %get-tuple-element.12.ids_ref, s32[2,4]{1,0:T(2,128)S(1)} %get-tuple-element.11.lens_ref, bf16[256,2560]{1,0:T(8,128)(2,1)S(1)} %copy-done.2, bf16[256,2560]{1,0:T(8,128)(2,1)S(1)} %copy-done.3, ...), custom_call_target="tpu_custom_call" | custom-call | tf_op jit(solution)/shard_map/pallas_call | solution.py:109
  97.2 0.1 slice.16
  97.3 1.7 slice.17
  99.1 1.5 pad_maximum_fusion
  100.6 6.4 %gather_fusion.1 = bf16[32,2,128,512]{3,2,1,0:T(8,128)(2,1)} fusion(bf16[8,2,128,512]{3,2,1,0:T(8,128)(2,1)} %pad_maximum_fusion, s32[1024]{0:T(1024)S(1)} %pad_clamp_fusion), kind=kCustom, calls=%fused_computation.1 | custom fusion | bytes 16777344 | tf_op jit(solution)/shard_map/jit(_take)/gather | solution.py:141
  107.0 11.0 %select_convert_fusion = bf16[32,2,128,512]{3,2,1,0:T(8,128)(2,1)} fusion(bf16[32,2,128,512]{3,2,1,0:T(8,128)(2,1)} %gather_fusion.1, pred[32]{0:T(512)(128)(4,1)S(1)} %compare_and_fusion, pred[32]{0:T(512)(128)(4,1)S(1)} %fusion), kind=kLoop, calls=%fused_computation.2 | loop fusion | flops 8388608 | bytes 16777280 | tf_op jit(solution)/shard_map/convert_element_type | solution.py:141
  118.0 0.0 reduce-scatter.2.cloned.1.call-update
  118.0 1.1 slice.26
  119.1 0.8 pad_maximum_fusion.1
  120.0 97.9 %reduce-scatter.2.cloned.1.call-done = bf16[1,2,128,512]{3,2,1,0:T(8,128)(2,1)} async-done(((bf16[32,2,128,512]{3,2,1,0:T(8,128)(2,1)}), bf16[1,2,128,512]{3,2,1,0:T(8,128)(2,1)}) %reduce-scatter.2.cloned.1.call-update) | async-done | bytes 262160 | tf_op jit(solution)/shard_map/reduce_scatter | solution.py:142
  (5 shorter events, 0.1 us)
Async XLA Ops:
  7.2 1.6 copy-start
  7.2 64.1 %all-gather.2.cloned.1.call-start = ((), (), s32[]{:S(2)}) async-start(), calls=%async_computation.1 | async-start | bytes 8650752 | tf_op jit(solution)/shard_map/all_gather | solution.py:120
  7.9 210.0 %reduce-scatter.2.cloned.1.call-start = ((), (), s32[]{:S(2)}) async-start(), calls=%async_computation.2 | async-start | bytes 8650752 | tf_op jit(solution)/shard_map/reduce_scatter | solution.py:142
  71.3 1.0 copy-start.1
  72.3 1.3 copy-start.2
  73.7 1.3 copy-start.3
Sparse Core Ops, SparseCore 0:
  10.5 60.7 all-gather.1
  118.1 99.7 reduce-scatter.1

commit v3 on v2

--- a/solution.py
+++ b/solution.py
@@ -22,7 +22,7 @@
 def attention_kernel(ids_ref, lens_ref, q_ref, do_ref, *refs):
     node_k = refs[0:DEPTH]
     node_v = refs[DEPTH : 2 * DEPTH]
-    own_k, own_v, dq_ref, dk_ref, dv_ref = refs[2 * DEPTH :]
+    own_k, own_v, dq_ref, own_out, sum_ref, keep_k, keep_v = refs[2 * DEPTH :]
     c = pl.program_id(1)
     factor = 1.0 / math.sqrt(HEAD_SIZE)
     key_block = jnp.concatenate([r[...] for r in node_k] + [own_k[...]], axis=0)
@@ -57,29 +57,29 @@
         dq_ref[:, cols] = dq[g * QUERY_LENGTH : (g + 1) * QUERY_LENGTH]
     dk = lax.dot_general(score_low, query_rows, tn, preferred_element_type=jnp.float32) * factor
     dv = lax.dot_general(probs_low, cot_rows, tn, preferred_element_type=jnp.float32)
+    own_out[0] = dk[NODE_ROWS:].astype(jnp.bfloat16)
+    own_out[1] = dv[NODE_ROWS:].astype(jnp.bfloat16)
 
     @pl.when(c == 0)
     def _():
-        dk_ref[0] = dk
-        dv_ref[0] = dv
+        keep_k[...] = dk[:NODE_ROWS]
+        keep_v[...] = dv[:NODE_ROWS]
 
     @pl.when(c == 1)
     def _():
+        sum_ref[...] = jnp.zeros(sum_ref.shape, sum_ref.dtype)
         for level_at in range(DEPTH):
             rows = slice(level_at * TILE_SLOTS, (level_at + 1) * TILE_SLOTS)
             same = ids_ref[0, level_at] == ids_ref[1, level_at]
-            for out_ref, term in ((dk_ref, dk), (dv_ref, dv)):
-                before = out_ref[0, rows, :]
-                here = term[rows]
+            for half, before, here in ((0, keep_k[rows, :], dk[rows]), (1, keep_v[rows, :], dv[rows])):
                 summed = before + here
-                out_ref[0, rows, :] = jnp.where(same, summed, before)
-                out_ref[1, rows, :] = jnp.where(same, summed, here)
-        dk_ref[1, NODE_ROWS:, :] = dk[NODE_ROWS:]
-        dv_ref[1, NODE_ROWS:, :] = dv[NODE_ROWS:]
+                sum_ref[ids_ref[0, level_at], half] = jnp.where(same, summed, before).astype(jnp.bfloat16)
+                sum_ref[ids_ref[1, level_at], half] = jnp.where(same, summed, here).astype(jnp.bfloat16)
 
 
 def attention(ids, lens, queries, cotangent, portion, suffix_key_value):
     members = ids.shape[0]
+    node_count = portion.shape[0]
     width = GROUP_SHARE * HEAD_SIZE
     row_block = pl.BlockSpec((QUERY_LENGTH, width), lambda h, c, ids, lens: (c, h))
 
@@ -92,7 +92,10 @@
     def own_block(half):
         return pl.BlockSpec((None, QUERY_LENGTH, HEAD_SIZE), lambda h, c, ids, lens: (half, c, h))
 
-    grad_block = pl.BlockSpec((members, KEY_ROWS, HEAD_SIZE), lambda h, c, ids, lens: (0, 0, h))
+    own_out_block = pl.BlockSpec((2, QUERY_LENGTH, HEAD_SIZE), lambda h, c, ids, lens: (0, c, h))
+    sum_block = pl.BlockSpec(
+        (node_count, 2, TILE_SLOTS, HEAD_SIZE), lambda h, c, ids, lens: (0, 0, 0, h)
+    )
     in_specs = (
         [row_block, row_block]
         + [node_block(level_at, 0) for level_at in range(DEPTH)]
@@ -103,42 +106,31 @@
         num_scalar_prefetch=2,
         grid=(KV_HEADS, members),
         in_specs=in_specs,
-        out_specs=[row_block, grad_block, grad_block],
+        out_specs=[row_block, own_out_block, sum_block],
+        scratch_shapes=[
+            pltpu.VMEM((NODE_ROWS, HEAD_SIZE), jnp.float32),
+            pltpu.VMEM((NODE_ROWS, HEAD_SIZE), jnp.float32),
+        ],
     )
-    grad_shape = jax.ShapeDtypeStruct((members, KEY_ROWS, KV_HEADS * HEAD_SIZE), jnp.float32)
     return pl.pallas_call(
         attention_kernel,
         grid_spec=grid_spec,
-        out_shape=[jax.ShapeDtypeStruct(queries.shape, jnp.bfloat16), grad_shape, grad_shape],
+        out_shape=[
+            jax.ShapeDtypeStruct(queries.shape, jnp.bfloat16),
+            jax.ShapeDtypeStruct(suffix_key_value.shape, jnp.bfloat16),
+            jax.ShapeDtypeStruct(portion.shape, jnp.bfloat16),
+        ],
         compiler_params=pltpu.CompilerParams(vmem_limit_bytes=48 * 1024 * 1024),
     )(ids, lens, queries, cotangent, *([portion] * (2 * DEPTH)), suffix_key_value, suffix_key_value)
 
 
 def body(queries, suffix_key_value, output_gradient, node_kv, paths, tile_lens):
-    members = paths.shape[0]
-    span_width = node_kv.shape[-1]
     portion = lax.all_gather(node_kv, "comp", axis=0, tiled=True)
-    node_count = portion.shape[0]
-    ids = jnp.clip(paths, 0, node_count - 1).astype(jnp.int32)
+    ids = jnp.clip(paths, 0, portion.shape[0] - 1).astype(jnp.int32)
     lens = jnp.take(tile_lens, ids).astype(jnp.int32)
-    query_out, key_gradient, value_gradient = attention(
+    query_out, suffix_out, block_sum = attention(
         ids, lens, queries, output_gradient, portion, suffix_key_value
     )
-    suffix_out = jnp.stack(
-        [key_gradient[:, NODE_ROWS:], value_gradient[:, NODE_ROWS:]], axis=0
-    ).reshape(2, members * QUERY_LENGTH, span_width).astype(jnp.bfloat16)
-    slots = ids.reshape(members * DEPTH)
-    hits = slots[None, :] == jnp.arange(node_count, dtype=jnp.int32)[:, None]
-    slot_of = jnp.argmax(hits, axis=1)
-    held = jnp.any(hits, axis=1)[:, None, None, None]
-    slot_grads = jnp.stack(
-        [
-            key_gradient[:, :NODE_ROWS].reshape(members * DEPTH, TILE_SLOTS, span_width),
-            value_gradient[:, :NODE_ROWS].reshape(members * DEPTH, TILE_SLOTS, span_width),
-        ],
-        axis=1,
-    )
-    block_sum = jnp.where(held, jnp.take(slot_grads, slot_of, axis=0), 0.0).astype(jnp.bfloat16)
     node_out = lax.psum_scatter(block_sum, "comp", scatter_dimension=0, tiled=True)
     return (query_out, suffix_out, node_out)
 

time: 225 us -> 205 us (0.911)
  other arithmetic: 15.5 us -> 0.7 us
  local copies, waits for them, and re-layouts: 13.9 us -> 3.46 us
  waiting for transfers between devices: 159 us -> 162 us
    convert_element_type x1 -> x0, other arithmetic: 11 us -> none  [body(): jnp.where(held, jnp.take(slot_grads, slot_of, axis=0), 0.0)]
    gather x1 -> x0, local copies, waits for them, and re-layouts: 6.38 us -> none  [body(): jnp.take(slot_grads, slot_of, axis=0)]
    another operation x3 -> x0, other arithmetic: 2.98 us -> none  [the longest x1 1.53 us: body(): jnp.stack([key_gradient[:, :NODE_ROWS].reshape(members * DEPTH, TILE_SLOT...]
    slice x4 -> x0, local copies, waits for them, and re-layouts: 2.98 us -> none  [the longest x1 1.73 us: body(): value_gradient[:, :NODE_ROWS]]
  transfers between devices with their start and end apart: 2 -> 2, of which waited for: 2 -> 2; matrix products, arithmetic and copies ran while one was open for 2% -> 1% of each run, Pallas kernels for 0% -> 0%
where the time goes in v3:
time: 205 us; the launch traced here: 204 us
  waiting for transfers between devices  162 us (79%)
  Pallas kernels  23.6 us (12%)
  between operations  14.1 us (7%)
  local copies, waits for them, and re-layouts  3.46 us (2%)
    reduce_scatter x1, waiting for transfers between devices, body(): lax.psum_scatter(block_sum, 'comp', scatter_dimension=0, tiled=True)  99.9 us
    all_gather x1, waiting for transfers between devices, body(): portion = lax.all_gather(node_kv, 'comp', axis=0, tiled=True)  61.8 us
    pallas_call x1, Pallas kernels, attention(): pl.pallas_call(attention_kernel, grid_spec=grid_spec, out_shape=[jax.Shap...  23.6 us
  transfers between devices with their start and end apart: 2, of which 2 were waited for; matrix products, arithmetic and copies ran while one was open for 1% of the time, Pallas kernels for 0%

profile of v3, /device:TPU:2, one launch (start us, length us, event | category | flops | bytes accessed | tf_op | source)
XLA Modules:
  0.0 204.3 jit_solution(7523976160959948115)
XLA Ops:
  7.2 0.0 copy-start
  7.2 0.0 copy-start.4
  7.2 0.0 copy-start.1
  7.2 0.0 all-gather.2.cloned.1.call-start
  7.2 0.7 all-gather.2.cloned.1.call-update
  7.9 0.0 reduce-scatter.2.cloned.1.call-start
  8.0 0.7 compare_select_fusion
  8.7 0.1 reshape.13
  8.8 0.0 copy-done
  8.8 0.6 gather_fusion
  9.4 0.1 reshape.12
  9.5 0.0 copy-done.4
  9.5 61.8 %all-gather.2.cloned.1.call-done.refs_0_.refs_1_.refs_2_.refs_3_.refs_4_.refs_5_.refs_6_.refs_7_ = bf16[32,2,128,512]{3,2,1,0:T(8,128)(2,1)} async-done(((bf16[1,2,128,512]{3,2,1,0:T(8,128)(2,1)}), bf16[32,2,128,512]{3,2,1,0:T(8,128)(2,1)}) %all-gather.2.cloned.1.call-update) | async-done | bytes 8388624 | tf_op jit(solution)/shard_map/all_gather | solution.py:128
  71.3 0.0 copy-done.1
  71.3 0.0 copy-start.2
  71.3 1.3 copy-done.2
  72.6 0.0 copy-start.3
  72.6 1.3 copy-done.3
  74.0 23.6 %shard_map.85 = (bf16[256,2560]{1,0:T(8,128)(2,1)}, bf16[2,256,512]{2,1,0:T(8,128)(2,1)}, bf16[32,2,128,512]{3,2,1,0:T(8,128)(2,1)}) custom-call(s32[2,4]{1,0:T(2,128)S(1)} %get-tuple-element.10.ids_ref, s32[2,4]{1,0:T(2,128)S(1)} %get-tuple-element.9.lens_ref, bf16[256,2560]{1,0:T(8,128)(2,1)S(1)} %copy-done.2, bf16[256,2560]{1,0:T(8,128)(2,1)S(1)} %copy-done.3, ...), custom_call_target="tpu_custom_call" | custom-call | tf_op jit(solution)/shard_map/pallas_call | solution.py:115
  97.6 0.0 reduce-scatter.2.cloned.1.call-update
  97.6 99.9 %reduce-scatter.2.cloned.1.call-done = bf16[1,2,128,512]{3,2,1,0:T(8,128)(2,1)} async-done(((bf16[32,2,128,512]{3,2,1,0:T(8,128)(2,1)}), bf16[1,2,128,512]{3,2,1,0:T(8,128)(2,1)}) %reduce-scatter.2.cloned.1.call-update) | async-done | bytes 262160 | tf_op jit(solution)/shard_map/reduce_scatter | solution.py:134
  (2 shorter events, 0.0 us)
Async XLA Ops:
  7.2 1.6 copy-start
  7.2 2.3 %copy-start.4 = (s32[2,4]{1,0:T(2,128)S(1)}, s32[2,4]{1,0:T(2,128)}, u32[]{:S(2)}) copy-start(s32[2,4]{1,0:T(2,128)} %param.10) | copy-start | bytes 100
  7.2 64.1 %copy-start.1 = (bf16[2,256,512]{2,1,0:T(8,128)(2,1)S(1)}, bf16[2,256,512]{2,1,0:T(8,128)(2,1)}, u32[]{:S(2)}) copy-start(bf16[2,256,512]{2,1,0:T(8,128)(2,1)} %refs_9_.1) | copy-start | bytes 1572868
  7.2 64.1 %all-gather.2.cloned.1.call-start = ((), (), s32[]{:S(2)}) async-start(), calls=%async_computation.1 | async-start | bytes 8650752 | tf_op jit(solution)/shard_map/all_gather | solution.py:128
  7.9 189.5 %reduce-scatter.2.cloned.1.call-start = ((), (), s32[]{:S(2)}) async-start(), calls=%async_computation.2 | async-start | bytes 8650752 | tf_op jit(solution)/shard_map/reduce_scatter | solution.py:134
  71.3 1.3 copy-start.2
  72.6 1.3 copy-start.3
Sparse Core Ops, SparseCore 0:
  10.6 60.7 all-gather.1
  97.7 99.6 reduce-scatter.1

commit v4 on v3

--- a/solution.py
+++ b/solution.py
@@ -131,7 +131,8 @@
     query_out, suffix_out, block_sum = attention(
         ids, lens, queries, output_gradient, portion, suffix_key_value
     )
-    node_out = lax.psum_scatter(block_sum, "comp", scatter_dimension=0, tiled=True)
+    received = lax.all_to_all(block_sum, "comp", 0, 0, tiled=True)
+    node_out = jnp.sum(received.astype(jnp.float32), axis=0, keepdims=True).astype(jnp.bfloat16)
     return (query_out, suffix_out, node_out)
 
 

time: 205 us -> 214 us (1.044)
  blocking collectives: 0 us -> 101 us
  waiting for transfers between devices: 162 us -> 61.9 us
  other arithmetic: 0.7 us -> 6.93 us
    all_to_all x0 -> x1, blocking collectives: none -> 101 us  [body(): received = lax.all_to_all(block_sum, 'comp', 0, 0, tiled=True)]
    reduce_scatter x1 -> x0, waiting for transfers between devices: 99.9 us -> none  [body(): lax.psum_scatter(block_sum, 'comp', scatter_dimension=0, tiled=True)]
    reduce_sum x0 -> x1, other arithmetic: none -> 5.54 us  [body(): jnp.sum(received.astype(jnp.float32), axis=0, keepdims=True)]
  transfers between devices with their start and end apart: 2 -> 1, of which waited for: 2 -> 1; matrix products, arithmetic and copies ran while one was open for 1% -> 1% of each run, Pallas kernels for 0% -> 0%
where the time goes in v4:
time: 214 us; the launch traced here: 211 us
  blocking collectives  101 us (47%)
  waiting for transfers between devices  61.9 us (29%)
  Pallas kernels  23.5 us (11%)
  between operations  14 us (7%)
  other arithmetic  6.93 us (3%)
  local copies, waits for them, and re-layouts  4.49 us (2%)
    all_to_all x1, blocking collectives, body(): received = lax.all_to_all(block_sum, 'comp', 0, 0, tiled=True)  101 us
    all_gather x1, waiting for transfers between devices, body(): portion = lax.all_gather(node_kv, 'comp', axis=0, tiled=True)  61.2 us
    pallas_call x1, Pallas kernels, attention(): pl.pallas_call(attention_kernel, grid_spec=grid_spec, out_shape=[jax.Shap...  23.5 us
    reduce_sum x1, other arithmetic, body(): jnp.sum(received.astype(jnp.float32), axis=0, keepdims=True)  5.54 us
  transfers between devices with their start and end apart: 1, of which 1 were waited for; matrix products, arithmetic and copies ran while one was open for 1% of the time, Pallas kernels for 0%

profile of v4, /device:TPU:2, one launch (start us, length us, event | category | flops | bytes accessed | tf_op | source)
XLA Modules:
  0.0 211.4 jit_solution(16664040034437348534)
XLA Ops:
  7.2 0.0 copy-start
  7.2 0.0 all-gather.2.cloned.1.call-start
  7.2 0.7 all-gather.2.cloned.1.call-update
  7.9 0.7 compare_select_fusion
  8.6 0.1 reshape.22
  8.7 0.0 copy-done
  8.7 0.6 gather_fusion
  9.3 0.1 reshape.21
  9.4 0.7 and_select_fusion
  10.1 61.2 %all-gather.2.cloned.1.call-done.refs_0_.refs_1_.refs_2_.refs_3_.refs_4_.refs_5_.refs_6_.refs_7_ = bf16[32,2,128,512]{3,2,1,0:T(8,128)(2,1)} async-done(((bf16[1,2,128,512]{3,2,1,0:T(8,128)(2,1)}), bf16[32,2,128,512]{3,2,1,0:T(8,128)(2,1)}) %all-gather.2.cloned.1.call-update) | async-done | bytes 8388624 | tf_op jit(solution)/shard_map/all_gather | solution.py:128
  71.3 0.0 copy-start.1
  71.3 1.0 copy-done.1
  72.3 0.0 copy-start.2
  72.3 1.3 copy-done.2
  73.7 0.0 copy-start.3
  73.7 1.3 copy-done.3
  75.0 23.5 %shard_map.85 = (bf16[256,2560]{1,0:T(8,128)(2,1)}, bf16[2,256,512]{2,1,0:T(8,128)(2,1)}, bf16[32,2,128,512]{3,2,1,0:T(8,128)(2,1)}) custom-call(s32[2,4]{1,0:T(2,128)S(1)} %get-tuple-element.10.ids_ref, s32[2,4]{1,0:T(2,128)S(1)} %get-tuple-element.9.lens_ref, bf16[256,2560]{1,0:T(8,128)(2,1)S(1)} %copy-done.2, bf16[256,2560]{1,0:T(8,128)(2,1)S(1)} %copy-done.3, ...), custom_call_target="tpu_custom_call" | custom-call | tf_op jit(solution)/shard_map/pallas_call | solution.py:115
  98.5 100.5 %all_to_all.5 = bf16[32,2,128,512]{3,2,1,0:T(8,128)(2,1)} all-to-all(bf16[32,2,128,512]{3,2,1,0:T(8,128)(2,1)} %get-tuple-element.8), channel_id=1, replica_groups=mesh['comp'=32,'prompt'=8] {'comp'}, dimensions={0} | all-to-all | bytes 16777216 | tf_op jit(solution)/shard_map/all_to_all | solution.py:134
  199.0 5.5 %reduce_sum.12 = bf16[2,128,512]{2,1,0:T(8,128)(2,1)} reduce(bf16[32,2,128,512]{3,2,1,0:T(8,128)(2,1)} %all_to_all.5, bf16[]{:T(256)} %constant.20.clone.1), dimensions={0}, to_apply=%region_0.1 | reduce | flops 4063232 | bytes 8650754 | tf_op jit(solution)/shard_map/reduce_sum | solution.py:135
  (1 shorter events, 0.0 us)
Async XLA Ops:
  7.2 1.5 copy-start
  7.2 64.1 %all-gather.2.cloned.1.call-start = ((), (), s32[]{:S(2)}) async-start(), calls=%async_computation.1 | async-start | bytes 8650752 | tf_op jit(solution)/shard_map/all_gather | solution.py:128
  71.3 1.0 copy-start.1
  72.3 1.3 copy-start.2
  73.7 1.3 copy-start.3
Sparse Core Ops, SparseCore 0:
  10.5 60.7 all-gather.1

commit v5 on v3

--- a/solution.py
+++ b/solution.py
@@ -19,7 +19,7 @@
 STACK_ROWS = GROUP_SHARE * QUERY_LENGTH
 
 
-def attention_kernel(ids_ref, lens_ref, q_ref, do_ref, *refs):
+def attention_kernel(ids_ref, lens_ref, bias_ref, q_ref, do_ref, *refs):
     node_k = refs[0:DEPTH]
     node_v = refs[DEPTH : 2 * DEPTH]
     own_k, own_v, dq_ref, own_out, sum_ref, keep_k, keep_v = refs[2 * DEPTH :]
@@ -30,23 +30,15 @@
     heads = [slice(g * HEAD_SIZE, (g + 1) * HEAD_SIZE) for g in range(GROUP_SHARE)]
     query_rows = jnp.concatenate([q_ref[:, cols] for cols in heads], axis=0)
     cot_rows = jnp.concatenate([do_ref[:, cols] for cols in heads], axis=0)
-    col = lax.broadcasted_iota(jnp.int32, (STACK_ROWS, KEY_ROWS), 1)
-    row = lax.broadcasted_iota(jnp.int32, (STACK_ROWS, KEY_ROWS), 0) % QUERY_LENGTH
-    level = col // TILE_SLOTS
-    slot = col % TILE_SLOTS
-    limit = jnp.where(
-        level == 0,
-        lens_ref[c, 0],
-        jnp.where(level == 1, lens_ref[c, 1], jnp.where(level == 2, lens_ref[c, 2], lens_ref[c, 3])),
-    )
-    visible = ((level < DEPTH) & (slot < limit)) | ((level >= DEPTH) & ((col - NODE_ROWS) <= row))
     nt = (((1,), (1,)), ((), ()))
     tn = (((0,), (0,)), ((), ()))
     scores = lax.dot_general(query_rows, key_block, nt, preferred_element_type=jnp.float32) * factor
-    scores = jnp.where(visible, scores, -jnp.inf)
+    scores = (scores.reshape(GROUP_SHARE, QUERY_LENGTH, KEY_ROWS) + bias_ref[...][None]).reshape(
+        STACK_ROWS, KEY_ROWS
+    )
     top = jnp.max(scores, axis=-1, keepdims=True)
     weights = jnp.exp(scores - top)
-    probs = weights / jnp.sum(weights, axis=-1, keepdims=True)
+    probs = weights * (1.0 / jnp.sum(weights, axis=-1, keepdims=True))
     probs_low = probs.astype(jnp.bfloat16)
     outputs = jnp.dot(probs_low, value_block, preferred_element_type=jnp.float32)
     centre = jnp.sum(cot_rows.astype(jnp.float32) * outputs, axis=-1, keepdims=True)
@@ -77,7 +69,7 @@
                 sum_ref[ids_ref[1, level_at], half] = jnp.where(same, summed, here).astype(jnp.bfloat16)
 
 
-def attention(ids, lens, queries, cotangent, portion, suffix_key_value):
+def attention(ids, lens, bias, queries, cotangent, portion, suffix_key_value):
     members = ids.shape[0]
     node_count = portion.shape[0]
     width = GROUP_SHARE * HEAD_SIZE
@@ -96,8 +88,9 @@
     sum_block = pl.BlockSpec(
         (node_count, 2, TILE_SLOTS, HEAD_SIZE), lambda h, c, ids, lens: (0, 0, 0, h)
     )
+    bias_block = pl.BlockSpec((None, QUERY_LENGTH, KEY_ROWS), lambda h, c, ids, lens: (c, 0, 0))
     in_specs = (
-        [row_block, row_block]
+        [bias_block, row_block, row_block]
         + [node_block(level_at, 0) for level_at in range(DEPTH)]
         + [node_block(level_at, 1) for level_at in range(DEPTH)]
         + [own_block(0), own_block(1)]
@@ -121,15 +114,27 @@
             jax.ShapeDtypeStruct(portion.shape, jnp.bfloat16),
         ],
         compiler_params=pltpu.CompilerParams(vmem_limit_bytes=48 * 1024 * 1024),
-    )(ids, lens, queries, cotangent, *([portion] * (2 * DEPTH)), suffix_key_value, suffix_key_value)
+    )(ids, lens, bias, queries, cotangent, *([portion] * (2 * DEPTH)), suffix_key_value, suffix_key_value)
 
 
 def body(queries, suffix_key_value, output_gradient, node_kv, paths, tile_lens):
     portion = lax.all_gather(node_kv, "comp", axis=0, tiled=True)
     ids = jnp.clip(paths, 0, portion.shape[0] - 1).astype(jnp.int32)
     lens = jnp.take(tile_lens, ids).astype(jnp.int32)
+    slot = jnp.arange(TILE_SLOTS, dtype=jnp.int32)
+    node_seen = (slot[None, None, :] < lens[:, :, None]).reshape(lens.shape[0], 1, NODE_ROWS)
+    own = jnp.arange(QUERY_LENGTH, dtype=jnp.int32)
+    causal = (own[None, :] <= own[:, None])[None]
+    visible = jnp.concatenate(
+        [
+            jnp.broadcast_to(node_seen, (lens.shape[0], QUERY_LENGTH, NODE_ROWS)),
+            jnp.broadcast_to(causal, (lens.shape[0], QUERY_LENGTH, QUERY_LENGTH)),
+        ],
+        axis=2,
+    )
+    bias = jnp.where(visible, 0.0, -jnp.inf).astype(jnp.float32)
     query_out, suffix_out, block_sum = attention(
-        ids, lens, queries, output_gradient, portion, suffix_key_value
+        ids, lens, bias, queries, output_gradient, portion, suffix_key_value
     )
     node_out = lax.psum_scatter(block_sum, "comp", scatter_dimension=0, tiled=True)
     return (query_out, suffix_out, node_out)

time: 205 us -> 204 us (level)
  no operation moved by 1% of the time
where the time goes in v5:
time: 204 us; the launch traced here: 203 us
  waiting for transfers between devices  162 us (79%)
  Pallas kernels  24 us (12%)
  between operations  14.1 us (7%)
  local copies, waits for them, and re-layouts  2.27 us (1%)
    reduce_scatter x1, waiting for transfers between devices, body(): lax.psum_scatter(block_sum, 'comp', scatter_dimension=0, tiled=True)  99.9 us
    all_gather x1, waiting for transfers between devices, body(): portion = lax.all_gather(node_kv, 'comp', axis=0, tiled=True)  61.6 us
    pallas_call x1, Pallas kernels, attention(): pl.pallas_call(attention_kernel, grid_spec=grid_spec, out_shape=[jax.Shap...  24 us
  transfers between devices with their start and end apart: 2, of which 2 were waited for; matrix products, arithmetic and copies ran while one was open for 1% of the time, Pallas kernels for 0%

profile of v5, /device:TPU:2, one launch (start us, length us, event | category | flops | bytes accessed | tf_op | source)
XLA Modules:
  0.0 203.4 jit_solution(10909612561432365507)
XLA Ops:
  7.2 0.0 copy-start
  7.2 0.0 copy-start.4
  7.2 0.0 copy-start.1
  7.2 0.0 copy-start.2
  7.2 0.0 all-gather.2.cloned.1.call-start
  7.3 0.7 all-gather.2.cloned.1.call-update
  7.9 0.0 reduce-scatter.2.cloned.1.call-start
  8.0 0.7 compare_select_fusion
  8.7 0.1 reshape.43
  8.8 0.0 copy-done
  8.8 0.6 gather_fusion
  9.4 0.1 reshape.42
  9.5 0.0 copy-done.4
  9.6 0.1 broadcast_bitcast_fusion
  9.7 0.1 add_select_fusion.bias_ref
  9.8 61.6 %all-gather.2.cloned.1.call-done.refs_0_.refs_1_.refs_2_.refs_3_.refs_4_.refs_5_.refs_6_.refs_7_ = bf16[32,2,128,512]{3,2,1,0:T(8,128)(2,1)} async-done(((bf16[1,2,128,512]{3,2,1,0:T(8,128)(2,1)}), bf16[32,2,128,512]{3,2,1,0:T(8,128)(2,1)}) %all-gather.2.cloned.1.call-update) | async-done | bytes 8388624 | tf_op jit(solution)/shard_map/all_gather | solution.py:121
  71.3 0.0 copy-done.1
  71.3 0.0 copy-done.2
  71.3 0.0 copy-start.3
  71.3 1.3 copy-done.3
  72.7 24.0 %shard_map.85 = (bf16[256,2560]{1,0:T(8,128)(2,1)}, bf16[2,256,512]{2,1,0:T(8,128)(2,1)}, bf16[32,2,128,512]{3,2,1,0:T(8,128)(2,1)}) custom-call(s32[2,4]{1,0:T(2,128)S(1)} %get-tuple-element.10.ids_ref, s32[2,4]{1,0:T(2,128)S(1)} %get-tuple-element.9.lens_ref, f32[2,128,640]{2,1,0:T(8,128)S(1)} %add_select_fusion.bias_ref, bf16[256,2560]{1,0:T(8,128)(2,1)S(1)} %copy-done.2, ...), custom_call_target="tpu_custom_call" | custom-call | tf_op jit(solution)/shard_map/pallas_call | solution.py:108
  96.7 0.0 reduce-scatter.2.cloned.1.call-update
  96.7 99.9 %reduce-scatter.2.cloned.1.call-done = bf16[1,2,128,512]{3,2,1,0:T(8,128)(2,1)} async-done(((bf16[32,2,128,512]{3,2,1,0:T(8,128)(2,1)}), bf16[1,2,128,512]{3,2,1,0:T(8,128)(2,1)}) %reduce-scatter.2.cloned.1.call-update) | async-done | bytes 262160 | tf_op jit(solution)/shard_map/reduce_scatter | solution.py:139
  (7 shorter events, 0.1 us)
Async XLA Ops:
  7.2 1.6 copy-start
  7.2 2.3 %copy-start.4 = (s32[2,4]{1,0:T(2,128)S(1)}, s32[2,4]{1,0:T(2,128)}, u32[]{:S(2)}) copy-start(s32[2,4]{1,0:T(2,128)} %param.10) | copy-start | bytes 100
  7.2 64.1 %copy-start.1 = (bf16[2,256,512]{2,1,0:T(8,128)(2,1)S(1)}, bf16[2,256,512]{2,1,0:T(8,128)(2,1)}, u32[]{:S(2)}) copy-start(bf16[2,256,512]{2,1,0:T(8,128)(2,1)} %refs_9_.1) | copy-start | bytes 1572868
  7.2 64.1 %copy-start.2 = (bf16[256,2560]{1,0:T(8,128)(2,1)S(1)}, bf16[256,2560]{1,0:T(8,128)(2,1)}, u32[]{:S(2)}) copy-start(bf16[256,2560]{1,0:T(8,128)(2,1)} %q_ref.1) | copy-start | bytes 3932164
  7.2 64.1 %all-gather.2.cloned.1.call-start = ((), (), s32[]{:S(2)}) async-start(), calls=%async_computation.1 | async-start | bytes 8650752 | tf_op jit(solution)/shard_map/all_gather | solution.py:121
  7.9 188.6 %reduce-scatter.2.cloned.1.call-start = ((), (), s32[]{:S(2)}) async-start(), calls=%async_computation.2 | async-start | bytes 8650752 | tf_op jit(solution)/shard_map/reduce_scatter | solution.py:139
  71.3 1.3 copy-start.3
Sparse Core Ops, SparseCore 0:
  10.6 60.7 all-gather.1
  96.8 99.6 reduce-scatter.1

commit v6 on v5

v6 whole, which is shorter than its diff:
```python
import math

import jax
import jax.numpy as jnp
from jax import lax
from jax.experimental import pallas as pl
from jax.experimental.pallas import tpu as pltpu
from jax.sharding import PartitionSpec as P

QUERY_HEADS = 20
KV_HEADS = 4
HEAD_SIZE = 128
TILE_SLOTS = 128
DEPTH = 4
QUERY_LENGTH = 128
GROUP_SHARE = QUERY_HEADS // KV_HEADS
NODE_ROWS = DEPTH * TILE_SLOTS
KEY_ROWS = NODE_ROWS + QUERY_LENGTH
STACK_ROWS = GROUP_SHARE * QUERY_LENGTH


HEADS_AT_ONCE = 2


def attention_kernel(ids_ref, lens_ref, bias_ref, q_ref, do_ref, *refs):
    node_k = refs[0:DEPTH]
    node_v = refs[DEPTH : 2 * DEPTH]
    own_k, own_v, dq_ref, own_out, sum_ref, keep_k, keep_v = refs[2 * DEPTH :]
    c = pl.program_id(1)
    factor = 1.0 / math.sqrt(HEAD_SIZE)
    nt = (((1,), (1,)), ((), ()))
    tn = (((0,), (0,)), ((), ()))
    bias = bias_ref[...][None]
    width = GROUP_SHARE * HEAD_SIZE
    grads = []
    for sub in range(HEADS_AT_ONCE):
        lanes = slice(sub * HEAD_SIZE, (sub + 1) * HEAD_SIZE)
        key_block = jnp.concatenate([r[:, lanes] for r in node_k] + [own_k[:, lanes]], axis=0)
        value_block = jnp.concatenate([r[:, lanes] for r in node_v] + [own_v[:, lanes]], axis=0)
        heads = [
            slice(sub * width + g * HEAD_SIZE, sub * width + (g + 1) * HEAD_SIZE)
            for g in range(GROUP_SHARE)
        ]
        query_rows = jnp.concatenate([q_ref[:, cols] for cols in heads], axis=0)
        cot_rows = jnp.concatenate([do_ref[:, cols] for cols in heads], axis=0)
        scores = lax.dot_general(query_rows, key_block, nt, preferred_element_type=jnp.float32) * factor
        scores = (scores.reshape(GROUP_SHARE, QUERY_LENGTH, KEY_ROWS) + bias).reshape(
            STACK_ROWS, KEY_ROWS
        )
        top = jnp.max(scores, axis=-1, keepdims=True)
        weights = jnp.exp(scores - top)
        probs = weights * (1.0 / jnp.sum(weights, axis=-1, keepdims=True))
        probs_low = probs.astype(jnp.bfloat16)
        outputs = jnp.dot(probs_low, value_block, preferred_element_type=jnp.float32)
        centre = jnp.sum(cot_rows.astype(jnp.float32) * outputs, axis=-1, keepdims=True)
        prob_grads = lax.dot_general(cot_rows, value_block, nt, preferred_element_type=jnp.float32)
        score_low = (probs * (prob_grads - centre)).astype(jnp.bfloat16)
        dq = (jnp.dot(score_low, key_block, preferred_element_type=jnp.float32) * factor).astype(
            jnp.bfloat16
        )
        for g, cols in enumerate(heads):
            dq_ref[:, cols] = dq[g * QUERY_LENGTH : (g + 1) * QUERY_LENGTH]
        dk = lax.dot_general(score_low, query_rows, tn, preferred_element_type=jnp.float32) * factor
        dv = lax.dot_general(probs_low, cot_rows, tn, preferred_element_type=jnp.float32)
        own_out[0, :, lanes] = dk[NODE_ROWS:].astype(jnp.bfloat16)
        own_out[1, :, lanes] = dv[NODE_ROWS:].astype(jnp.bfloat16)
        grads.append((lanes, dk, dv))

    @pl.when(c == 0)
    def _():
        for lanes, dk, dv in grads:
            keep_k[:, lanes] = dk[:NODE_ROWS]
            keep_v[:, lanes] = dv[:NODE_ROWS]

    @pl.when(c == 1)
    def _():
        sum_ref[...] = jnp.zeros(sum_ref.shape, sum_ref.dtype)
        for level_at in range(DEPTH):
            rows = slice(level_at * TILE_SLOTS, (level_at + 1) * TILE_SLOTS)
            same = ids_ref[0, level_at] == ids_ref[1, level_at]
            for lanes, dk, dv in grads:
                for half, before, here in (
                    (0, keep_k[rows, lanes], dk[rows]),
                    (1, keep_v[rows, lanes], dv[rows]),
                ):
                    summed = before + here
                    sum_ref[ids_ref[0, level_at], half, :, lanes] = jnp.where(
                        same, summed, before
                    ).astype(jnp.bfloat16)
                    sum_ref[ids_ref[1, level_at], half, :, lanes] = jnp.where(
                        same, summed, here
                    ).astype(jnp.bfloat16)


def attention(ids, lens, bias, queries, cotangent, portion, suffix_key_value):
    members = ids.shape[0]
    node_count = portion.shape[0]
    width = HEADS_AT_ONCE * GROUP_SHARE * HEAD_SIZE
    lanes = HEADS_AT_ONCE * HEAD_SIZE
    row_block = pl.BlockSpec((QUERY_LENGTH, width), lambda h, c, ids, lens: (c, h))

    def node_block(level_at, half):
        return pl.BlockSpec(
            (None, None, TILE_SLOTS, lanes),
            lambda h, c, ids, lens: (ids[c, level_at], half, 0, h),
        )

    def own_block(half):
        return pl.BlockSpec((None, QUERY_LENGTH, lanes), lambda h, c, ids, lens: (half, c, h))

    own_out_block = pl.BlockSpec((2, QUERY_LENGTH, lanes), lambda h, c, ids, lens: (0, c, h))
    sum_block = pl.BlockSpec((node_count, 2, TILE_SLOTS, lanes), lambda h, c, ids, lens: (0, 0, 0, h))
    bias_block = pl.BlockSpec((None, QUERY_LENGTH, KEY_ROWS), lambda h, c, ids, lens: (c, 0, 0))
    in_specs = (
        [bias_block, row_block, row_block]
        + [node_block(level_at, 0) for level_at in range(DEPTH)]
        + [node_block(level_at, 1) for level_at in range(DEPTH)]
        + [own_block(0), own_block(1)]
    )
    grid_spec = pltpu.PrefetchScalarGridSpec(
        num_scalar_prefetch=2,
        grid=(KV_HEADS // HEADS_AT_ONCE, members),
        in_specs=in_specs,
        out_specs=[row_block, own_out_block, sum_block],
        scratch_shapes=[
            pltpu.VMEM((NODE_ROWS, lanes), jnp.float32),
            pltpu.VMEM((NODE_ROWS, lanes), jnp.float32),
        ],
    )
    return pl.pallas_call(
        attention_kernel,
        grid_spec=grid_spec,
        out_shape=[
            jax.ShapeDtypeStruct(queries.shape, jnp.bfloat16),
            jax.ShapeDtypeStruct(suffix_key_value.shape, jnp.bfloat16),
            jax.ShapeDtypeStruct(portion.shape, jnp.bfloat16),
        ],
        compiler_params=pltpu.CompilerParams(vmem_limit_bytes=56 * 1024 * 1024),
    )(ids, lens, bias, queries, cotangent, *([portion] * (2 * DEPTH)), suffix_key_value, suffix_key_value)


def body(queries, suffix_key_value, output_gradient, node_kv, paths, tile_lens):
    portion = lax.all_gather(node_kv, "comp", axis=0, tiled=True)
    ids = jnp.clip(paths, 0, portion.shape[0] - 1).astype(jnp.int32)
    lens = jnp.take(tile_lens, ids).astype(jnp.int32)
    slot = jnp.arange(TILE_SLOTS, dtype=jnp.int32)
    node_seen = (slot[None, None, :] < lens[:, :, None]).reshape(lens.shape[0], 1, NODE_ROWS)
    own = jnp.arange(QUERY_LENGTH, dtype=jnp.int32)
    causal = (own[None, :] <= own[:, None])[None]
    visible = jnp.concatenate(
        [
            jnp.broadcast_to(node_seen, (lens.shape[0], QUERY_LENGTH, NODE_ROWS)),
            jnp.broadcast_to(causal, (lens.shape[0], QUERY_LENGTH, QUERY_LENGTH)),
        ],
        axis=2,
    )
    bias = jnp.where(visible, 0.0, -jnp.inf).astype(jnp.float32)
    query_out, suffix_out, block_sum = attention(
        ids, lens, bias, queries, output_gradient, portion, suffix_key_value
    )
    node_out = lax.psum_scatter(block_sum, "comp", scatter_dimension=0, tiled=True)
    return (query_out, suffix_out, node_out)


def solution(mesh):
    rows = ("prompt", "comp")
    in_specs = (
        P(rows, None),
        P(None, rows, None),
        P(rows, None),
        P(rows, None, None, None),
        P(rows, None),
        P("prompt"),
    )
    out_specs = (
        P(rows, None),
        P(None, rows, None),
        P(rows, None, None, None),
    )
    return jax.shard_map(body, mesh=mesh, in_specs=in_specs, out_specs=out_specs, check_vma=False)
```

time: 204 us -> 200 us (0.980)
  Pallas kernels: 24 us -> 21.7 us
    pallas_call x1, Pallas kernels: 24 us -> 21.7 us  [attention(): pl.pallas_call(attention_kernel, grid_spec=grid_spec, out_shape=[jax.Shap...]
  transfers between devices with their start and end apart: 2 -> 2, of which waited for: 2 -> 2; matrix products, arithmetic and copies ran while one was open for 1% -> 2% of each run, Pallas kernels for 0% -> 0%
where the time goes in v6:
time: 200 us
  waiting for transfers between devices  161 us (80%)
  Pallas kernels  21.7 us (11%)
  between operations  14.1 us (7%)
  other arithmetic  2.2 us (1%)
    reduce_scatter x1, waiting for transfers between devices, body(): lax.psum_scatter(block_sum, 'comp', scatter_dimension=0, tiled=True)  99.9 us
    all_gather x1, waiting for transfers between devices, body(): portion = lax.all_gather(node_kv, 'comp', axis=0, tiled=True)  60.2 us
    pallas_call x1, Pallas kernels, attention(): pl.pallas_call(attention_kernel, grid_spec=grid_spec, out_shape=[jax.Shap...  21.7 us
  transfers between devices with their start and end apart: 2, of which 2 were waited for; matrix products, arithmetic and copies ran while one was open for 2% of the time, Pallas kernels for 0%

profile of v6, /device:TPU:2, one launch (start us, length us, event | category | flops | bytes accessed | tf_op | source)
XLA Modules:
  0.0 199.8 jit_solution(13743329982433182893)
XLA Ops:
  7.2 0.0 copy-start
  7.2 0.0 copy-start.2
  7.2 0.0 all-gather.2.cloned.1.call-start
  7.2 0.7 all-gather.2.cloned.1.call-update
  7.9 0.0 reduce-scatter.2.cloned.1.call-start
  8.0 0.7 compare_select_fusion
  8.7 0.1 reshape.43
  8.7 0.0 copy-done
  8.8 0.6 gather_fusion
  9.4 0.1 reshape.42
  9.5 0.0 copy-done.2
  9.5 0.6 and_select_fusion
  10.1 0.0 copy-start.1
  10.1 0.1 broadcast_bitcast_fusion
  10.2 0.9 add_select_fusion.bias_ref
  11.1 60.2 %all-gather.2.cloned.1.call-done.refs_0_.refs_1_.refs_2_.refs_3_.refs_4_.refs_5_.refs_6_.refs_7_ = bf16[32,2,128,512]{3,2,1,0:T(8,128)(2,1)} async-done(((bf16[1,2,128,512]{3,2,1,0:T(8,128)(2,1)}), bf16[32,2,128,512]{3,2,1,0:T(8,128)(2,1)}) %all-gather.2.cloned.1.call-update) | async-done | bytes 8388624 | tf_op jit(solution)/shard_map/all_gather | solution.py:143
  71.3 0.0 copy-done.1
  71.3 21.7 %shard_map.85 = (bf16[256,2560]{1,0:T(8,128)(2,1)}, bf16[2,256,512]{2,1,0:T(8,128)(2,1)}, bf16[32,2,128,512]{3,2,1,0:T(8,128)(2,1)}) custom-call(s32[2,4]{1,0:T(2,128)} %get-tuple-element.10.ids_ref, s32[2,4]{1,0:T(2,128)} %copy-done.1, f32[2,128,640]{2,1,0:T(8,128)} %add_select_fusion.bias_ref, bf16[256,2560]{1,0:T(8,128)(2,1)} %q_ref.1, ...), custom_call_target="tpu_custom_call" | custom-call | tf_op jit(solution)/shard_map/pallas_call | solution.py:130
  93.0 0.0 reduce-scatter.2.cloned.1.call-update
  93.1 99.9 %reduce-scatter.2.cloned.1.call-done = bf16[1,2,128,512]{3,2,1,0:T(8,128)(2,1)} async-done(((bf16[32,2,128,512]{3,2,1,0:T(8,128)(2,1)}), bf16[1,2,128,512]{3,2,1,0:T(8,128)(2,1)}) %reduce-scatter.2.cloned.1.call-update) | async-done | bytes 262160 | tf_op jit(solution)/shard_map/reduce_scatter | solution.py:161
  (6 shorter events, 0.1 us)
Async XLA Ops:
  7.2 1.6 copy-start
  7.2 2.3 %copy-start.2 = (s32[2,4]{1,0:T(2,128)S(1)}, s32[2,4]{1,0:T(2,128)}, u32[]{:S(2)}) copy-start(s32[2,4]{1,0:T(2,128)} %param.10) | copy-start | bytes 100
  7.2 64.1 %all-gather.2.cloned.1.call-start = ((), (), s32[]{:S(2)}) async-start(), calls=%async_computation.1 | async-start | bytes 8650752 | tf_op jit(solution)/shard_map/all_gather | solution.py:143
  7.9 185.1 %reduce-scatter.2.cloned.1.call-start = ((), (), s32[]{:S(2)}) async-start(), calls=%async_computation.2 | async-start | bytes 8650752 | tf_op jit(solution)/shard_map/reduce_scatter | solution.py:161
  10.1 61.2 %copy-start.1 = (s32[2,4]{1,0:T(2,128)}, s32[2,4]{1,0:T(2,128)S(1)}, u32[]{:S(2)}) copy-start(s32[2,4]{1,0:T(2,128)S(1)} %get-tuple-element.9.lens_ref) | copy-start | bytes 100
Sparse Core Ops, SparseCore 0:
  10.5 60.7 all-gather.1
  93.2 99.7 reduce-scatter.1

commit v7 on v6

--- a/solution.py
+++ b/solution.py
@@ -19,7 +19,7 @@
 STACK_ROWS = GROUP_SHARE * QUERY_LENGTH
 
 
-HEADS_AT_ONCE = 2
+HEADS_AT_ONCE = 4
 
 
 def attention_kernel(ids_ref, lens_ref, bias_ref, q_ref, do_ref, *refs):

time: 200 us -> 200 us (level)
  no operation moved by 1% of the time
where the time goes in v7:
time: 200 us
  waiting for transfers between devices  161 us (80%)
  Pallas kernels  22.2 us (11%)
  between operations  14.1 us (7%)
  other arithmetic  2.2 us (1%)
    reduce_scatter x1, waiting for transfers between devices, body(): lax.psum_scatter(block_sum, 'comp', scatter_dimension=0, tiled=True)  99.9 us
    all_gather x1, waiting for transfers between devices, body(): portion = lax.all_gather(node_kv, 'comp', axis=0, tiled=True)  60.2 us
    pallas_call x1, Pallas kernels, attention(): pl.pallas_call(attention_kernel, grid_spec=grid_spec, out_shape=[jax.Shap...  22.2 us
  transfers between devices with their start and end apart: 2, of which 2 were waited for; matrix products, arithmetic and copies ran while one was open for 2% of the time, Pallas kernels for 0%

profile of v7, /device:TPU:2, one launch (start us, length us, event | category | flops | bytes accessed | tf_op | source)
XLA Modules:
  0.0 200.2 jit_solution(10517681820610573717)
XLA Ops:
  7.2 0.0 copy-start
  7.2 0.0 copy-start.2
  7.2 0.0 all-gather.2.cloned.1.call-start
  7.2 0.7 all-gather.2.cloned.1.call-update
  7.9 0.0 reduce-scatter.2.cloned.1.call-start
  8.0 0.7 compare_select_fusion
  8.7 0.1 reshape.43
  8.7 0.0 copy-done
  8.8 0.6 gather_fusion
  9.4 0.1 reshape.42
  9.5 0.0 copy-done.2
  9.5 0.6 and_select_fusion
  10.1 0.0 copy-start.1
  10.1 0.1 broadcast_bitcast_fusion
  10.2 0.9 add_select_fusion.bias_ref
  11.1 60.2 %all-gather.2.cloned.1.call-done.refs_0_.refs_1_.refs_2_.refs_3_.refs_4_.refs_5_.refs_6_.refs_7_ = bf16[32,2,128,512]{3,2,1,0:T(8,128)(2,1)} async-done(((bf16[1,2,128,512]{3,2,1,0:T(8,128)(2,1)}), bf16[32,2,128,512]{3,2,1,0:T(8,128)(2,1)}) %all-gather.2.cloned.1.call-update) | async-done | bytes 8388624 | tf_op jit(solution)/shard_map/all_gather | solution.py:143
  71.3 0.0 copy-done.1
  71.3 22.2 %shard_map.85 = (bf16[256,2560]{1,0:T(8,128)(2,1)}, bf16[2,256,512]{2,1,0:T(8,128)(2,1)}, bf16[32,2,128,512]{3,2,1,0:T(8,128)(2,1)}) custom-call(s32[2,4]{1,0:T(2,128)} %get-tuple-element.10.ids_ref, s32[2,4]{1,0:T(2,128)} %copy-done.1, f32[2,128,640]{2,1,0:T(8,128)} %add_select_fusion.bias_ref, bf16[256,2560]{1,0:T(8,128)(2,1)} %q_ref.1, ...), custom_call_target="tpu_custom_call" | custom-call | tf_op jit(solution)/shard_map/pallas_call | solution.py:130
  93.5 0.0 reduce-scatter.2.cloned.1.call-update
  93.5 99.9 %reduce-scatter.2.cloned.1.call-done = bf16[1,2,128,512]{3,2,1,0:T(8,128)(2,1)} async-done(((bf16[32,2,128,512]{3,2,1,0:T(8,128)(2,1)}), bf16[1,2,128,512]{3,2,1,0:T(8,128)(2,1)}) %reduce-scatter.2.cloned.1.call-update) | async-done | bytes 262160 | tf_op jit(solution)/shard_map/reduce_scatter | solution.py:161
  (6 shorter events, 0.1 us)
Async XLA Ops:
  7.2 1.6 copy-start
  7.2 2.3 %copy-start.2 = (s32[2,4]{1,0:T(2,128)S(1)}, s32[2,4]{1,0:T(2,128)}, u32[]{:S(2)}) copy-start(s32[2,4]{1,0:T(2,128)} %param.10) | copy-start | bytes 100
  7.2 64.1 %all-gather.2.cloned.1.call-start = ((), (), s32[]{:S(2)}) async-start(), calls=%async_computation.1 | async-start | bytes 8650752 | tf_op jit(solution)/shard_map/all_gather | solution.py:143
  7.9 185.5 %reduce-scatter.2.cloned.1.call-start = ((), (), s32[]{:S(2)}) async-start(), calls=%async_computation.2 | async-start | bytes 8650752 | tf_op jit(solution)/shard_map/reduce_scatter | solution.py:161
  10.1 61.2 %copy-start.1 = (s32[2,4]{1,0:T(2,128)}, s32[2,4]{1,0:T(2,128)S(1)}, u32[]{:S(2)}) copy-start(s32[2,4]{1,0:T(2,128)S(1)} %get-tuple-element.9.lens_ref) | copy-start | bytes 100
Sparse Core Ops, SparseCore 0:
  10.5 60.7 all-gather.1
  93.7 99.6 reduce-scatter.1
